TPU v7x, 512 devices: a whole 4x4x16 slice. The times are simulated.
512 devices in a mesh: band: 8 (over x_lo, y), xy: 64 (over z, x_hi, core).
Axes of the slice: x: 4 (x_hi: 2, x_lo: 2; x = x_hi * 2 + x_lo), y: 4, z: 16, core: 2. Of those that a mesh axis runs over, the one named last changes fastest.
Arguments:
- orbitals: float32 [16, 64, 128, 256], P('band', 'xy'), may hold values from -6 to 6
- energies: float32 [16], P('band'), may hold values from -1.5 to -0.25
- occupation: int32 [16], P('band'), may hold values from 1 to 2
- potential: float32 [64, 128, 256], P('xy'), may hold values from 0.25 to 2
- trials: float32 [4, 64, 128, 256], P(None, 'xy'), may hold values from -8 to 23
Outputs:
- density: float32 [4, 64, 128, 256], P(None, 'xy', 'band')
- response_matrix: float32 [4, 4], replicated
All inputs are finite; a program needn't handle non-finite values.
Results may differ from a plain program's by a relative error of at most 0.0001.
Values sent between devices are 32-bit elements; how exact they have to be, the bound alone decides.
No kernel may reach another device: no remote copies, remote signals or barrier semaphores. Data moves between devices by JAX's collectives and lax.ppermute only.
A program may use at most 64 MiB of HBM per device.

v0:
```python
import math

import jax
import jax.numpy as jnp
from jax import lax
from jax.sharding import PartitionSpec as P

ITERS = 3


def padded_2(block, sides, width):
    for axis, dim in sides:
        count = lax.axis_size(axis)
        forward = [(i, i + 1) for i in range(count - 1)]
        forward.append((count - 1, 0))
        backward = [(target, source) for source, target in forward]
        low = lax.ppermute(
            lax.slice_in_dim(block, block.shape[dim] - width, None, axis=dim), axis, forward
        )
        high = lax.ppermute(lax.slice_in_dim(block, 0, width, axis=dim), axis, backward)
        block = jnp.concatenate([low, block, high], axis=dim)
    return block


def respond(psi_rows, energy_rows, weight_rows, potential_part, trial_part, project, apply_op):
    orbital_count, cell_count = psi_rows.shape
    trial_count = trial_part.shape[0]
    row_count = orbital_count * trial_count
    diagonal_op = 3.0 + potential_part.reshape(1, 1, cell_count) - energy_rows[:, None, None]
    diagonal_op = jnp.broadcast_to(diagonal_op, (orbital_count, trial_count, cell_count)).reshape(
        row_count, cell_count
    )
    products = trial_part[None, :, :] * psi_rows[:, None, :]
    right_side = -project(products.reshape(row_count, cell_count))
    update = project(right_side / diagonal_op)
    for iteration in range(ITERS):
        residual = right_side - apply_op(update, diagonal_op)
        update = update + project(residual / diagonal_op)
    weights = weight_rows[:, None, None] * psi_rows[:, None, :]
    return jnp.sum(weights * update.reshape(orbital_count, trial_count, cell_count), axis=0)


def neighbours_z(field_block):
    z_padded = jnp.pad(field_block, ((0, 0), (0, 0), (0, 0), (1, 1)))
    return z_padded[..., 2:] + z_padded[..., :-2]


def local(orbitals, energies, occupation, potential, trials):
    nb_dev, width_x, width_y, width_z = orbitals.shape
    trial_count = trials.shape[0]
    cell_count = width_x * width_y * width_z
    cell_total = cell_count * lax.axis_size("xy")
    orbital_total = nb_dev * lax.axis_size("band")
    y_share = width_y // lax.axis_size("band")
    band_index = lax.axis_index("band")
    highest = lax.Precision.HIGHEST
    trial_slice = lax.dynamic_slice_in_dim(trials, band_index * y_share, y_share, 2)
    psi_flat = orbitals.reshape(nb_dev, cell_count)
    psi_all = lax.all_gather(psi_flat, "band", axis=0, tiled=True)

    def project_slab(vectors):
        intersection = jnp.dot(
            psi_all, vectors.T, precision=highest, preferred_element_type=jnp.float32
        )
        intersection = lax.psum(intersection, "xy") / cell_total
        return vectors - jnp.dot(
            intersection.T, psi_all, precision=highest, preferred_element_type=jnp.float32
        )

    def apply_slab(vectors, diagonal_op):
        field_block = vectors.reshape(-1, width_x, width_y, width_z)
        padded = padded_2(field_block, (("xy", 1),), 1)
        beside = padded[:, 2:] + padded[:, :-2]
        beside = beside + jnp.roll(field_block, 1, 2) + jnp.roll(field_block, -1, 2)
        beside = beside + neighbours_z(field_block)
        return diagonal_op * vectors - 0.5 * beside.reshape(vectors.shape)

    summed = respond(
        psi_flat,
        energies,
        occupation.astype(jnp.float32),
        potential.reshape(cell_count),
        trials.reshape(trial_count, cell_count),
        project_slab,
        apply_slab,
    )
    partial_grid = (summed / math.sqrt(orbital_total)).reshape(
        trial_count, width_x, width_y, width_z
    )
    density = lax.psum_scatter(partial_grid, "band", scatter_dimension=2, tiled=True)
    local_sum = jnp.dot(
        density.reshape(trial_count, -1),
        trial_slice.reshape(trial_count, -1).T,
        precision=highest,
        preferred_element_type=jnp.float32,
    )
    response_matrix = lax.psum(local_sum, ("band", "xy")) / cell_total
    return (density, response_matrix)


def solution(mesh):
    in_specs = (
        P("band", "xy", None, None),
        P("band"),
        P("band"),
        P("xy", None, None),
        P(None, "xy", None, None),
    )
    out_specs = (P(None, "xy", "band", None), P())
    return jax.shard_map(local, mesh=mesh, in_specs=in_specs, out_specs=out_specs, check_vma=False)
```

profile of v0, /device:TPU:1, one launch (start us, length us, event | category | flops | bytes accessed | tf_op | source)
XLA Modules:
  0.0 987.3 jit_solution(15164408557984125261)
XLA Ops:
  7.2 0.0 all-gather.3.cloned.1.call-start
  7.2 1.8 reshape.121
  9.0 0.0 all-gather.3.cloned.1.call-update
  9.1 0.0 reduce-scatter.2.cloned.1.call-start
  9.1 0.9 add_bitcast_fusion
  10.0 0.0 copy-start.11
  10.0 0.1 copy.13
  10.1 0.0 copy-start.12
  10.1 0.9 broadcast_subtract_fusion
  11.0 0.2 broadcast_in_dim.2
  11.2 0.4 reshape.114
  11.6 0.2 copy.11
  11.8 0.3 copy.12
  12.1 0.2 broadcast_multiply_fusion
  12.4 1.4 mul.77
  13.7 45.2 %all-gather.3.cloned.1.call-done = f32[8,2,32768]{2,1,0:T(2,128)} async-done(((f32[1,2,32768]{2,1,0:T(2,128)}), f32[8,2,32768]{2,1,0:T(2,128)}) %all-gather.3.cloned.1.call-update) | async-done | bytes 2097168 | tf_op jit(solution)/shard_map/all_gather | solution.py:59
  58.9 2.7 reshape.122
  61.6 3.8 convolution_bitcast_fusion.4
  65.4 135.0 %psum.42 = f32[16,8]{0,1:T(8,128)S(1)} all-reduce(f32[16,8]{0,1:T(8,128)S(1)} %convolution_bitcast_fusion.4), channel_id=1, replica_groups=mesh['band'=8,'xy'=64] {'xy'}, use_global_device_ids=true, to_apply=%region_0.0 | all-reduce | flops 128 | bytes 1024 | tf_op jit(solution)/shard_map/psum | solution.py:65
  200.4 3.4 fusion.40
  203.9 1.0 copy-done.6
  204.8 2.5 convolution_bitcast_fusion.3
  207.4 128.3 %psum.43 = f32[16,8]{0,1:T(8,128)S(1)} all-reduce(f32[16,8]{0,1:T(8,128)S(1)} %convolution_bitcast_fusion.3), channel_id=1, replica_groups=mesh['band'=8,'xy'=64] {'xy'}, use_global_device_ids=true, to_apply=%region_1.0 | all-reduce | flops 128 | bytes 1024 | tf_op jit(solution)/shard_map/psum | solution.py:65
  335.7 2.3 convolution_subtract_fusion.3
  338.0 2.9 collective-permute-start
  340.9 4.4 collective-permute-start.1
  345.3 0.1 fusion.38
  345.4 21.4 %collective-permute-done = f32[8,1,128,256]{3,0,2,1:T(8,128)S(1)} collective-permute-done((f32[8,1,128,256]{3,0,2,1:T(8,128)S(1)}, f32[8,1,128,256]{3,0,2,1:T(8,128)S(1)}, u32[]{:S(2)}, u32[]{:S(2)}) %collective-permute-start) | collective-permute-done | bytes 1048608 | tf_op jit(solution)/shard_map/ppermute | solution.py:20
  366.9 0.0 collective-permute-done.1
  366.9 0.6 fusion.6
  367.5 1.0 copy-done.8
  368.5 2.7 convolution_bitcast_fusion.2
  371.2 124.7 %psum.44 = f32[16,8]{0,1:T(8,128)S(1)} all-reduce(f32[16,8]{0,1:T(8,128)S(1)} %convolution_bitcast_fusion.2), channel_id=1, replica_groups=mesh['band'=8,'xy'=64] {'xy'}, use_global_device_ids=true, to_apply=%region_2.3 | all-reduce | flops 128 | bytes 1024 | tf_op jit(solution)/shard_map/psum | solution.py:65
  495.9 3.1 fusion.2
  499.1 6.5 collective-permute-start.2
  505.5 1.9 collective-permute-start.3
  507.5 0.1 fusion.36
  507.7 20.3 %collective-permute-done.2 = f32[8,1,128,256]{3,0,2,1:T(8,128)S(1)} collective-permute-done((f32[8,1,128,256]{3,0,2,1:T(8,128)S(1)}, f32[8,1,128,256]{3,0,2,1:T(8,128)S(1)}, u32[]{:S(2)}, u32[]{:S(2)}) %collective-permute-start.2) | collective-permute-done | bytes 1048608 | tf_op jit(solution)/shard_map/ppermute | solution.py:20
  527.9 0.6 fusion.9
  528.6 1.0 copy-done.9
  529.6 2.7 convolution_bitcast_fusion.1
  532.3 127.0 %psum.45 = f32[16,8]{0,1:T(8,128)S(1)} all-reduce(f32[16,8]{0,1:T(8,128)S(1)} %convolution_bitcast_fusion.1), channel_id=1, replica_groups=mesh['band'=8,'xy'=64] {'xy'}, use_global_device_ids=true, to_apply=%region_3.4 | all-reduce | flops 128 | bytes 1024 | tf_op jit(solution)/shard_map/psum | solution.py:65
  659.3 3.1 fusion.1
  662.4 4.2 collective-permute-start.4
  666.6 2.9 collective-permute-start.5
  669.5 0.9 broadcast_multiply_fusion.2
  670.3 0.1 fusion.34
  670.5 20.8 %collective-permute-done.4 = f32[8,1,128,256]{3,0,2,1:T(8,128)S(1)} collective-permute-done((f32[8,1,128,256]{3,0,2,1:T(8,128)S(1)}, f32[8,1,128,256]{3,0,2,1:T(8,128)S(1)}, u32[]{:S(2)}, u32[]{:S(2)}) %collective-permute-start.4) | collective-permute-done | bytes 1048608 | tf_op jit(solution)/shard_map/ppermute | solution.py:20
  691.3 0.0 collective-permute-done.5
  691.3 0.6 fusion.12
  691.9 1.0 copy-done.7
  692.9 2.7 convolution_bitcast_fusion
  695.6 124.9 %psum.46 = f32[16,8]{0,1:T(8,128)S(1)} all-reduce(f32[16,8]{0,1:T(8,128)S(1)} %convolution_bitcast_fusion), channel_id=1, replica_groups=mesh['band'=8,'xy'=64] {'xy'}, use_global_device_ids=true, to_apply=%region_4.5 | all-reduce | flops 128 | bytes 1024 | tf_op jit(solution)/shard_map/psum | solution.py:65
  820.5 4.1 fusion
  824.7 1.6 reshape.118
  826.2 0.4 multiply_reduce_fusion
  826.7 0.1 broadcast_multiply_fusion.1
  826.8 0.9 copy.22
  827.7 0.0 reduce-scatter.2.cloned.1.call-update
  827.7 0.9 constant_dynamic-slice_fusion
  828.6 41.6 %reduce-scatter.2.cloned.1.call-done = f32[4,1,16,256]{3,2,1,0:T(8,128)} async-done(((f32[4,1,128,256]{3,2,1,0:T(8,128)}), f32[4,1,16,256]{3,2,1,0:T(8,128)}) %reduce-scatter.2.cloned.1.call-update) | async-done | bytes 65552 | tf_op jit(solution)/shard_map/reduce_scatter | solution.py:90
  870.1 1.2 convolution_bitcast_fusion.5
  871.4 108.6 %psum.47 = f32[4,4]{1,0:T(4,128)S(1)} all-reduce(f32[4,4]{1,0:T(4,128)S(1)} %convolution_bitcast_fusion.5), channel_id=1, replica_groups=mesh['band'=8,'xy'=64] {'band','xy'}, use_global_device_ids=true, to_apply=%region_7.8 | all-reduce | flops 16 | bytes 128 | tf_op jit(solution)/shard_map/psum | solution.py:97
  979.9 0.6 broadcast_multiply_fusion.3
  (27 shorter events, 0.1 us)
Async XLA Ops:
  7.2 51.8 %all-gather.3.cloned.1.call-start = ((), (), s32[]{:S(2)}) async-start(), calls=%async_computation.2 | async-start | bytes 2359296 | tf_op jit(solution)/shard_map/all_gather | solution.py:59
  9.1 861.1 %reduce-scatter.2.cloned.1.call-start = ((), (), s32[]{:S(2)}) async-start(), calls=%async_computation.1 | async-start | bytes 589824 | tf_op jit(solution)/shard_map/reduce_scatter | solution.py:90
  10.0 1.5 copy-start.11
  10.1 1.7 copy-start.12
  203.9 1.0 copy-start.6
  338.0 29.5 %copy-start.5 = (f32[8,32768]{1,0:T(8,128)}, f32[8,32768]{1,0:T(8,128)S(1)}, u32[]{:S(2)}) copy-start(f32[8,32768]{1,0:T(8,128)S(1)} %convolution_subtract_fusion.3) | copy-start | bytes 3145732
  338.0 28.9 %collective-permute-start = (f32[8,1,128,256]{3,0,2,1:T(8,128)S(1)}, f32[8,1,128,256]{3,0,2,1:T(8,128)S(1)}, u32[]{:S(2)}, u32[]{:S(2)}) collective-permute-start(f32[8,1,128,256]{3,0,2,1:T(8,128)S(1)} %bitcast.60), channel_id=1, source_target_pairs={{1,0},{2,1},{3,2},{4,3},{5,4},{6,5},{7,6},{8,7},{9,8},{10,9},{11,1... | collective-permute-start | bytes 3145736 | tf_op jit(solution)/shard_map/ppermute | solution.py:20
  340.9 26.0 %collective-permute-start.1 = (f32[8,1,128,256]{3,0,2,1:T(8,128)S(1)}, f32[8,1,128,256]{3,0,2,1:T(8,128)S(1)}, u32[]{:S(2)}, u32[]{:S(2)}) collective-permute-start(f32[8,1,128,256]{3,0,2,1:T(8,128)S(1)} %bitcast.61), channel_id=1, source_target_pairs={{0,1},{1,2},{2,3},{3,4},{4,5},{5,6},{6,7},{7,8},{8,9},{9,10},{10,1... | collective-permute-start | bytes 3145736 | tf_op jit(solution)/shard_map/ppermute | solution.py:17
  366.9 1.7 copy-start
  367.5 1.0 copy-start.8
  495.9 11.6 %copy-start.13 = (s32[2]{0:T(128)S(1)}, s32[2]{0:T(128)}, u32[]{:S(2)}) copy-start(s32[2]{0:T(128)} %param.7) | copy-start | bytes 28
  499.1 29.5 %copy-start.4 = (f32[8,32768]{1,0:T(8,128)}, f32[8,32768]{1,0:T(8,128)S(1)}, u32[]{:S(2)}) copy-start(f32[8,32768]{1,0:T(8,128)S(1)} %fusion.2) | copy-start | bytes 3145732
  499.1 28.9 %collective-permute-start.2 = (f32[8,1,128,256]{3,0,2,1:T(8,128)S(1)}, f32[8,1,128,256]{3,0,2,1:T(8,128)S(1)}, u32[]{:S(2)}, u32[]{:S(2)}) collective-permute-start(f32[8,1,128,256]{3,0,2,1:T(8,128)S(1)} %bitcast.55), channel_id=1, source_target_pairs={{1,0},{2,1},{3,2},{4,3},{5,4},{6,5},{7,6},{8,7},{9,8},{10,9},{11,1... | collective-permute-start | bytes 3145736 | tf_op jit(solution)/shard_map/ppermute | solution.py:20
  505.5 22.4 %collective-permute-start.3 = (f32[8,1,128,256]{3,0,2,1:T(8,128)S(1)}, f32[8,1,128,256]{3,0,2,1:T(8,128)S(1)}, u32[]{:S(2)}, u32[]{:S(2)}) collective-permute-start(f32[8,1,128,256]{3,0,2,1:T(8,128)S(1)} %bitcast.56), channel_id=1, source_target_pairs={{0,1},{1,2},{2,3},{3,4},{4,5},{5,6},{6,7},{7,8},{8,9},{9,10},{10,1... | collective-permute-start | bytes 3145736 | tf_op jit(solution)/shard_map/ppermute | solution.py:17
  527.9 1.7 copy-start.1
  528.6 1.0 copy-start.9
  662.4 29.5 %copy-start.3 = (f32[8,32768]{1,0:T(8,128)}, f32[8,32768]{1,0:T(8,128)S(1)}, u32[]{:S(2)}) copy-start(f32[8,32768]{1,0:T(8,128)S(1)} %fusion.1) | copy-start | bytes 3145732
  662.4 28.9 %collective-permute-start.4 = (f32[8,1,128,256]{3,0,2,1:T(8,128)S(1)}, f32[8,1,128,256]{3,0,2,1:T(8,128)S(1)}, u32[]{:S(2)}, u32[]{:S(2)}) collective-permute-start(f32[8,1,128,256]{3,0,2,1:T(8,128)S(1)} %bitcast.50), channel_id=1, source_target_pairs={{1,0},{2,1},{3,2},{4,3},{5,4},{6,5},{7,6},{8,7},{9,8},{10,9},{11,1... | collective-permute-start | bytes 3145736 | tf_op jit(solution)/shard_map/ppermute | solution.py:20
  666.6 24.7 %collective-permute-start.5 = (f32[8,1,128,256]{3,0,2,1:T(8,128)S(1)}, f32[8,1,128,256]{3,0,2,1:T(8,128)S(1)}, u32[]{:S(2)}, u32[]{:S(2)}) collective-permute-start(f32[8,1,128,256]{3,0,2,1:T(8,128)S(1)} %bitcast.51), channel_id=1, source_target_pairs={{0,1},{1,2},{2,3},{3,4},{4,5},{5,6},{6,7},{7,8},{8,9},{9,10},{10,1... | collective-permute-start | bytes 3145736 | tf_op jit(solution)/shard_map/ppermute | solution.py:17
  691.3 1.7 copy-start.2
  691.9 1.0 copy-start.7
  824.7 1.6 copy-start.10
Sparse Core Ops, SparseCore 0:
  10.0 48.8 all-gather.2
  827.8 42.2 reduce-scatter.1
where the time goes:
time: 988 us; the launch traced here: 987 us
  blocking collectives  749 us (76%)
  waiting for transfers between devices  149 us (15%)
  matrix products  31.7 us (3%)
  starting transfers between devices  22.8 us (2%)
  local copies, waits for them, and re-layouts  14.8 us (1%)
  between operations  14.4 us (1%)
    psum x5, blocking collectives, project_slab(): intersection = lax.psum(intersection, 'xy') / cell_total  640 us
    psum x1, blocking collectives, local(): response_matrix = lax.psum(local_sum, ('band', 'xy')) / cell_total  109 us
    ppermute x3, waiting for transfers between devices, padded_2(): lax.ppermute(lax.slice_in_dim(block, 0, width, axis=dim), axis, backward)  62.5 us
    all_gather x1, waiting for transfers between devices, local(): psi_all = lax.all_gather(psi_flat, 'band', axis=0, tiled=True)  45.2 us
    reduce_scatter x1, waiting for transfers between devices, local(): lax.psum_scatter(partial_grid, 'band', scatter_dimension=2, tiled=True)  41.6 us
  transfers between devices with their start and end apart: 8, of which 5 were waited for; matrix products, arithmetic and copies ran while one was open for 1% of the time, Pallas kernels for 0%

commit v1 on v0

--- a/solution.py
+++ b/solution.py
@@ -20,6 +20,17 @@
         high = lax.ppermute(lax.slice_in_dim(block, 0, width, axis=dim), axis, backward)
         block = jnp.concatenate([low, block, high], axis=dim)
     return block
+
+
+def tree_sum(value, axes):
+    for axis in axes:
+        count = lax.axis_size(axis)
+        step = 1
+        while step < count:
+            pairs = [(i, i ^ step) for i in range(count)]
+            value = value + lax.ppermute(value, axis, pairs)
+            step *= 2
+    return value
 
 
 def respond(psi_rows, energy_rows, weight_rows, potential_part, trial_part, project, apply_op):
@@ -62,7 +73,7 @@
         intersection = jnp.dot(
             psi_all, vectors.T, precision=highest, preferred_element_type=jnp.float32
         )
-        intersection = lax.psum(intersection, "xy") / cell_total
+        intersection = tree_sum(intersection, ("xy",)) / cell_total
         return vectors - jnp.dot(
             intersection.T, psi_all, precision=highest, preferred_element_type=jnp.float32
         )
@@ -94,7 +105,7 @@
         precision=highest,
         preferred_element_type=jnp.float32,
     )
-    response_matrix = lax.psum(local_sum, ("band", "xy")) / cell_total
+    response_matrix = tree_sum(local_sum, ("band", "xy")) / cell_total
     return (density, response_matrix)
 
 

time: 988 us -> 522 us (0.53)
  blocking collectives: 749 us -> 0 us
  starting transfers between devices: 22.8 us -> 247 us
  waiting for transfers between devices: 149 us -> 214 us
    psum x6 -> x0, blocking collectives: 749 us -> none  [the longest x5 640 us: project_slab(): intersection = lax.psum(intersection, 'xy') / cell_total]
    ppermute x0 -> x39, starting transfers between devices: none -> 212 us  [tree_sum(): value = value + lax.ppermute(value, axis, pairs)]
    ppermute x0 -> x39, waiting for transfers between devices: none -> 60.2 us  [tree_sum(): value = value + lax.ppermute(value, axis, pairs)]
  transfers between devices with their start and end apart: 8 -> 47, of which waited for: 5 -> 43; matrix products, arithmetic and copies ran while one was open for 1% -> 2% of each run, Pallas kernels for 0% -> 0%
where the time goes in v1:
time: 522 us; the launch traced here: 516 us
  starting transfers between devices  247 us (47%)
  waiting for transfers between devices  214 us (41%)
  matrix products  22.8 us (4%)
  between operations  14.7 us (3%)
  local copies, waits for them, and re-layouts  14 us (3%)
    ppermute x39, starting transfers between devices, tree_sum(): value = value + lax.ppermute(value, axis, pairs)  212 us
    ppermute x3, waiting for transfers between devices, padded_2(): lax.ppermute(lax.slice_in_dim(block, 0, width, axis=dim), axis, backward)  64.7 us
    ppermute x39, waiting for transfers between devices, tree_sum(): value = value + lax.ppermute(value, axis, pairs)  60.2 us
    all_gather x1, waiting for transfers between devices, local(): psi_all = lax.all_gather(psi_flat, 'band', axis=0, tiled=True)  46.7 us
    reduce_scatter x1, waiting for transfers between devices, local(): lax.psum_scatter(partial_grid, 'band', scatter_dimension=2, tiled=True)  42 us
    ppermute x3, starting transfers between devices, padded_2(): lax.ppermute(lax.slice_in_dim(block, 0, width, axis=dim), axis, backward)  23.3 us
    dot_general x5, matrix products, project_slab(): jnp.dot(psi_all, vectors.T, precision=highest, preferred_element_type=jnp...  13.1 us
    ppermute x3, starting transfers between devices, padded_2(): lax.ppermute(lax.slice_in_dim(block, block.shape[dim] - width, None, axis...  11.6 us
  transfers between devices with their start and end apart: 47, of which 43 were waited for; matrix products, arithmetic and copies ran while one was open for 2% of the time, Pallas kernels for 0%

profile of v1, /device:TPU:1, one launch (start us, length us, event | category | flops | bytes accessed | tf_op | source)
XLA Modules:
  0.0 516.0 jit_solution(7207219664055754807)
XLA Ops:
  12.3 46.7 %all-gather.3.cloned.1.call-done = f32[8,2,32768]{2,1,0:T(2,128)} async-done(((f32[1,2,32768]{2,1,0:T(2,128)}), f32[8,2,32768]{2,1,0:T(2,128)}) %all-gather.3.cloned.1.call-update) | async-done | bytes 2097168 | tf_op jit(solution)/shard_map/all_gather | solution.py:70
  58.9 2.7 reshape.122
  61.7 2.5 convolution_bitcast_fusion.4
  64.2 7.9 %collective-permute-start = (f32[16,8]{0,1:T(8,128)S(1)}, f32[16,8]{0,1:T(8,128)S(1)}, u32[]{:S(2)}, u32[]{:S(2)}) collective-permute-start(f32[16,8]{0,1:T(8,128)S(1)} %convolution_bitcast_fusion.4), channel_id=1, source_target_pairs={{0,1},{1,0},{2,3},{3,2},{4,5},{5,4},{6,7},{7,6},{8,9},{9,8},{10,11... | collective-permute-start | bytes 1544 | tf_op jit(solution)/shard_map/ppermute | solution.py:31
  72.9 4.3 collective-permute-start.1
  78.8 3.2 collective-permute-start.2
  83.1 4.2 collective-permute-start.3
  88.4 7.4 %collective-permute-start.4 = (f32[16,8]{0,1:T(8,128)S(1)}, f32[16,8]{0,1:T(8,128)S(1)}, u32[]{:S(2)}, u32[]{:S(2)}) collective-permute-start(f32[16,8]{0,1:T(8,128)S(1)} %add.199), channel_id=1, source_target_pairs={{0,16},{1,17},{2,18},{3,19},{4,20},{5,21},{6,22},{7,23},{8,24},{9,... | collective-permute-start | bytes 1544 | tf_op jit(solution)/shard_map/ppermute | solution.py:31
  96.7 12.4 %collective-permute-start.5 = (f32[16,8]{0,1:T(8,128)S(1)}, f32[16,8]{0,1:T(8,128)S(1)}, u32[]{:S(2)}, u32[]{:S(2)}) collective-permute-start(f32[16,8]{0,1:T(8,128)S(1)} %add.200), channel_id=1, source_target_pairs={{0,32},{1,33},{2,34},{3,35},{4,36},{5,37},{6,38},{7,39},{8,40},{9,... | collective-permute-start | bytes 1544 | tf_op jit(solution)/shard_map/ppermute | solution.py:31
  112.1 2.5 fusion.45
  114.6 2.5 convolution_bitcast_fusion.3
  117.1 7.1 %collective-permute-start.6 = (f32[16,8]{0,1:T(8,128)S(1)}, f32[16,8]{0,1:T(8,128)S(1)}, u32[]{:S(2)}, u32[]{:S(2)}) collective-permute-start(f32[16,8]{0,1:T(8,128)S(1)} %convolution_bitcast_fusion.3), channel_id=1, source_target_pairs={{0,1},{1,0},{2,3},{3,2},{4,5},{5,4},{6,7},{7,6},{8,9},{9,8},{10,11... | collective-permute-start | bytes 1544 | tf_op jit(solution)/shard_map/ppermute | solution.py:31
  125.1 4.3 collective-permute-start.7
  130.9 2.3 collective-permute-start.8
  135.3 2.6 collective-permute-start.9
  137.9 2.6 collective-permute-done.9
  140.5 5.8 %collective-permute-start.10 = (f32[16,8]{0,1:T(8,128)S(1)}, f32[16,8]{0,1:T(8,128)S(1)}, u32[]{:S(2)}, u32[]{:S(2)}) collective-permute-start(f32[16,8]{0,1:T(8,128)S(1)} %add.208), channel_id=1, source_target_pairs={{0,16},{1,17},{2,18},{3,19},{4,20},{5,21},{6,22},{7,23},{8,24},{9,... | collective-permute-start | bytes 1544 | tf_op jit(solution)/shard_map/ppermute | solution.py:31
  146.3 2.5 collective-permute-done.10
  148.8 10.9 %collective-permute-start.11 = (f32[16,8]{0,1:T(8,128)S(1)}, f32[16,8]{0,1:T(8,128)S(1)}, u32[]{:S(2)}, u32[]{:S(2)}) collective-permute-start(f32[16,8]{0,1:T(8,128)S(1)} %add.209), channel_id=1, source_target_pairs={{0,32},{1,33},{2,34},{3,35},{4,36},{5,37},{6,38},{7,39},{8,40},{9,... | collective-permute-start | bytes 1544 | tf_op jit(solution)/shard_map/ppermute | solution.py:31
  159.7 2.1 collective-permute-done.11
  163.0 8.0 %collective-permute-start.12 = (f32[8,1,128,256]{3,0,2,1:T(8,128)S(1)}, f32[8,1,128,256]{3,0,2,1:T(8,128)S(1)}, u32[]{:S(2)}, u32[]{:S(2)}) collective-permute-start(f32[8,1,128,256]{3,0,2,1:T(8,128)S(1)} %bitcast.55), channel_id=1, source_target_pairs={{1,0},{2,1},{3,2},{4,3},{5,4},{6,5},{7,6},{8,7},{9,8},{10,9},{11,1... | collective-permute-start | bytes 3145736 | tf_op jit(solution)/shard_map/ppermute | solution.py:20
  171.0 4.4 collective-permute-start.13
  175.5 21.4 %collective-permute-done.12 = f32[8,1,128,256]{3,0,2,1:T(8,128)S(1)} collective-permute-done((f32[8,1,128,256]{3,0,2,1:T(8,128)S(1)}, f32[8,1,128,256]{3,0,2,1:T(8,128)S(1)}, u32[]{:S(2)}, u32[]{:S(2)}) %collective-permute-start.12) | collective-permute-done | bytes 1048608 | tf_op jit(solution)/shard_map/ppermute | solution.py:20
  197.6 2.7 convolution_bitcast_fusion.2
  203.4 2.9 collective-permute-start.15
  206.3 2.9 collective-permute-done.15
  209.2 2.3 collective-permute-start.16
  213.6 2.6 collective-permute-start.17
  216.2 2.6 collective-permute-done.17
  218.8 5.8 %collective-permute-start.18 = (f32[16,8]{0,1:T(8,128)S(1)}, f32[16,8]{0,1:T(8,128)S(1)}, u32[]{:S(2)}, u32[]{:S(2)}) collective-permute-start(f32[16,8]{0,1:T(8,128)S(1)} %add.219), channel_id=1, source_target_pairs={{0,16},{1,17},{2,18},{3,19},{4,20},{5,21},{6,22},{7,23},{8,24},{9,... | collective-permute-start | bytes 1544 | tf_op jit(solution)/shard_map/ppermute | solution.py:31
  224.6 2.5 collective-permute-done.18
  227.1 10.9 %collective-permute-start.19 = (f32[16,8]{0,1:T(8,128)S(1)}, f32[16,8]{0,1:T(8,128)S(1)}, u32[]{:S(2)}, u32[]{:S(2)}) collective-permute-start(f32[16,8]{0,1:T(8,128)S(1)} %add.220), channel_id=1, source_target_pairs={{0,32},{1,33},{2,34},{3,35},{4,36},{5,37},{6,38},{7,39},{8,40},{9,... | collective-permute-start | bytes 1544 | tf_op jit(solution)/shard_map/ppermute | solution.py:31
  241.4 7.8 %collective-permute-start.20 = (f32[8,1,128,256]{3,0,2,1:T(8,128)S(1)}, f32[8,1,128,256]{3,0,2,1:T(8,128)S(1)}, u32[]{:S(2)}, u32[]{:S(2)}) collective-permute-start(f32[8,1,128,256]{3,0,2,1:T(8,128)S(1)} %bitcast.60), channel_id=1, source_target_pairs={{1,0},{2,1},{3,2},{4,3},{5,4},{6,5},{7,6},{8,7},{9,8},{10,9},{11,1... | collective-permute-start | bytes 3145736 | tf_op jit(solution)/shard_map/ppermute | solution.py:20
  249.2 3.0 collective-permute-start.21
  252.4 21.6 %collective-permute-done.20 = f32[8,1,128,256]{3,0,2,1:T(8,128)S(1)} collective-permute-done((f32[8,1,128,256]{3,0,2,1:T(8,128)S(1)}, f32[8,1,128,256]{3,0,2,1:T(8,128)S(1)}, u32[]{:S(2)}, u32[]{:S(2)}) %collective-permute-start.20) | collective-permute-done | bytes 1048608 | tf_op jit(solution)/shard_map/ppermute | solution.py:20
  274.6 2.7 convolution_bitcast_fusion.1
  280.4 4.1 collective-permute-start.23
  286.2 3.3 collective-permute-start.24
  290.6 4.5 collective-permute-start.25
  296.1 7.4 %collective-permute-start.26 = (f32[16,8]{0,1:T(8,128)S(1)}, f32[16,8]{0,1:T(8,128)S(1)}, u32[]{:S(2)}, u32[]{:S(2)}) collective-permute-start(f32[16,8]{0,1:T(8,128)S(1)} %add.231), channel_id=1, source_target_pairs={{0,16},{1,17},{2,18},{3,19},{4,20},{5,21},{6,22},{7,23},{8,24},{9,... | collective-permute-start | bytes 1544 | tf_op jit(solution)/shard_map/ppermute | solution.py:31
  304.4 10.6 %collective-permute-start.27 = (f32[16,8]{0,1:T(8,128)S(1)}, f32[16,8]{0,1:T(8,128)S(1)}, u32[]{:S(2)}, u32[]{:S(2)}) collective-permute-start(f32[16,8]{0,1:T(8,128)S(1)} %add.232), channel_id=1, source_target_pairs={{0,32},{1,33},{2,34},{3,35},{4,36},{5,37},{6,38},{7,39},{8,40},{9,... | collective-permute-start | bytes 1544 | tf_op jit(solution)/shard_map/ppermute | solution.py:31
  315.0 2.5 collective-permute-done.27
  318.8 7.5 %collective-permute-start.28 = (f32[8,1,128,256]{3,0,2,1:T(8,128)S(1)}, f32[8,1,128,256]{3,0,2,1:T(8,128)S(1)}, u32[]{:S(2)}, u32[]{:S(2)}) collective-permute-start(f32[8,1,128,256]{3,0,2,1:T(8,128)S(1)} %bitcast.50), channel_id=1, source_target_pairs={{1,0},{2,1},{3,2},{4,3},{5,4},{6,5},{7,6},{8,7},{9,8},{10,9},{11,1... | collective-permute-start | bytes 3145736 | tf_op jit(solution)/shard_map/ppermute | solution.py:20
  326.2 4.2 collective-permute-start.29
  330.6 21.6 %collective-permute-done.28 = f32[8,1,128,256]{3,0,2,1:T(8,128)S(1)} collective-permute-done((f32[8,1,128,256]{3,0,2,1:T(8,128)S(1)}, f32[8,1,128,256]{3,0,2,1:T(8,128)S(1)}, u32[]{:S(2)}, u32[]{:S(2)}) %collective-permute-start.28) | collective-permute-done | bytes 1048608 | tf_op jit(solution)/shard_map/ppermute | solution.py:20
  352.9 2.7 convolution_bitcast_fusion
  355.6 2.1 collective-permute-start.30
  358.6 4.0 collective-permute-start.31
  364.5 3.3 collective-permute-start.32
  368.8 4.5 collective-permute-start.33
  374.3 7.4 %collective-permute-start.34 = (f32[16,8]{0,1:T(8,128)S(1)}, f32[16,8]{0,1:T(8,128)S(1)}, u32[]{:S(2)}, u32[]{:S(2)}) collective-permute-start(f32[16,8]{0,1:T(8,128)S(1)} %add.243), channel_id=1, source_target_pairs={{0,16},{1,17},{2,18},{3,19},{4,20},{5,21},{6,22},{7,23},{8,24},{9,... | collective-permute-start | bytes 1544 | tf_op jit(solution)/shard_map/ppermute | solution.py:31
  382.7 10.6 %collective-permute-start.35 = (f32[16,8]{0,1:T(8,128)S(1)}, f32[16,8]{0,1:T(8,128)S(1)}, u32[]{:S(2)}, u32[]{:S(2)}) collective-permute-start(f32[16,8]{0,1:T(8,128)S(1)} %add.244), channel_id=1, source_target_pairs={{0,32},{1,33},{2,34},{3,35},{4,36},{5,37},{6,38},{7,39},{8,40},{9,... | collective-permute-start | bytes 1544 | tf_op jit(solution)/shard_map/ppermute | solution.py:31
  395.7 2.3 fusion
  401.9 42.0 %reduce-scatter.2.cloned.1.call-done = f32[4,1,16,256]{3,2,1,0:T(8,128)} async-done(((f32[4,1,128,256]{3,2,1,0:T(8,128)}), f32[4,1,16,256]{3,2,1,0:T(8,128)}) %reduce-scatter.2.cloned.1.call-update) | async-done | bytes 65552 | tf_op jit(solution)/shard_map/reduce_scatter | solution.py:101
  447.1 2.4 collective-permute-done.36
  449.5 2.4 collective-permute-start.37
  451.9 3.4 collective-permute-done.37
  455.4 2.4 collective-permute-start.38
  459.7 11.0 %collective-permute-start.39 = (f32[4,4]{1,0:T(4,128)S(1)}, f32[4,4]{1,0:T(4,128)S(1)}, u32[]{:S(2)}, u32[]{:S(2)}) collective-permute-start(f32[4,4]{1,0:T(4,128)S(1)} %add.250), channel_id=1, source_target_pairs={{0,1},{1,0},{2,3},{3,2},{4,5},{5,4},{6,7},{7,6},{8,9},{9,8},{10,11... | collective-permute-start | bytes 200 | tf_op jit(solution)/shard_map/ppermute | solution.py:31
  471.5 4.3 collective-permute-start.40
  477.4 3.1 collective-permute-start.41
  481.7 4.2 collective-permute-start.42
  486.9 7.3 %collective-permute-start.43 = (f32[4,4]{1,0:T(4,128)S(1)}, f32[4,4]{1,0:T(4,128)S(1)}, u32[]{:S(2)}, u32[]{:S(2)}) collective-permute-start(f32[4,4]{1,0:T(4,128)S(1)} %add.254), channel_id=1, source_target_pairs={{0,16},{1,17},{2,18},{3,19},{4,20},{5,21},{6,22},{7,23},{8,24},{9,... | collective-permute-start | bytes 200 | tf_op jit(solution)/shard_map/ppermute | solution.py:31
  495.2 12.4 %collective-permute-start.44 = (f32[4,4]{1,0:T(4,128)S(1)}, f32[4,4]{1,0:T(4,128)S(1)}, u32[]{:S(2)}, u32[]{:S(2)}) collective-permute-start(f32[4,4]{1,0:T(4,128)S(1)} %add.255), channel_id=1, source_target_pairs={{0,32},{1,33},{2,34},{3,35},{4,36},{5,37},{6,38},{7,39},{8,40},{9,... | collective-permute-start | bytes 200 | tf_op jit(solution)/shard_map/ppermute | solution.py:31
  (114 shorter events, 63.3 us)
Async XLA Ops:
  7.2 51.8 %all-gather.3.cloned.1.call-start = ((), (), s32[]{:S(2)}) async-start(), calls=%async_computation.2 | async-start | bytes 2359296 | tf_op jit(solution)/shard_map/all_gather | solution.py:70
  9.0 434.9 %reduce-scatter.2.cloned.1.call-start = ((), (), s32[]{:S(2)}) async-start(), calls=%async_computation.1 | async-start | bytes 589824 | tf_op jit(solution)/shard_map/reduce_scatter | solution.py:101
  12.2 97.1 %copy-start = (f32[8,32768]{1,0:T(8,128)}, f32[8,32768]{1,0:T(8,128)S(1)}, u32[]{:S(2)}) copy-start(f32[8,32768]{1,0:T(8,128)S(1)} %mul.77) | copy-start | bytes 3145732
  61.6 34.1 %copy-start.2 = (f32[1,128,256]{2,1,0:T(8,128)S(1)}, f32[1,128,256]{2,1,0:T(8,128)}, u32[]{:S(2)}) copy-start(f32[1,128,256]{2,1,0:T(8,128)} %param.8) | copy-start | bytes 393220
  61.6 47.5 %copy-start.3 = (f32[2]{0:T(128)S(1)}, f32[2]{0:T(128)}, u32[]{:S(2)}) copy-start(f32[2]{0:T(128)} %param.6) | copy-start | bytes 28
  64.2 8.7 %collective-permute-start = (f32[16,8]{0,1:T(8,128)S(1)}, f32[16,8]{0,1:T(8,128)S(1)}, u32[]{:S(2)}, u32[]{:S(2)}) collective-permute-start(f32[16,8]{0,1:T(8,128)S(1)} %convolution_bitcast_fusion.4), channel_id=1, source_target_pairs={{0,1},{1,0},{2,3},{3,2},{4,5},{5,4},{6,7},{7,6},{8,9},{9,8},{10,11... | collective-permute-start | bytes 1544 | tf_op jit(solution)/shard_map/ppermute | solution.py:31
  72.9 5.8 %collective-permute-start.1 = (f32[16,8]{0,1:T(8,128)S(1)}, f32[16,8]{0,1:T(8,128)S(1)}, u32[]{:S(2)}, u32[]{:S(2)}) collective-permute-start(f32[16,8]{0,1:T(8,128)S(1)} %add.196), channel_id=1, source_target_pairs={{0,2},{1,3},{2,0},{3,1},{4,6},{5,7},{6,4},{7,5},{8,10},{9,11},{10,... | collective-permute-start | bytes 1544 | tf_op jit(solution)/shard_map/ppermute | solution.py:31
  78.8 4.3 collective-permute-start.2
  83.1 5.2 %collective-permute-start.3 = (f32[16,8]{0,1:T(8,128)S(1)}, f32[16,8]{0,1:T(8,128)S(1)}, u32[]{:S(2)}, u32[]{:S(2)}) collective-permute-start(f32[16,8]{0,1:T(8,128)S(1)} %add.198), channel_id=1, source_target_pairs={{0,8},{1,9},{2,10},{3,11},{4,12},{5,13},{6,14},{7,15},{8,0},{9,1},... | collective-permute-start | bytes 1544 | tf_op jit(solution)/shard_map/ppermute | solution.py:31
  88.4 8.3 %collective-permute-start.4 = (f32[16,8]{0,1:T(8,128)S(1)}, f32[16,8]{0,1:T(8,128)S(1)}, u32[]{:S(2)}, u32[]{:S(2)}) collective-permute-start(f32[16,8]{0,1:T(8,128)S(1)} %add.199), channel_id=1, source_target_pairs={{0,16},{1,17},{2,18},{3,19},{4,20},{5,21},{6,22},{7,23},{8,24},{9,... | collective-permute-start | bytes 1544 | tf_op jit(solution)/shard_map/ppermute | solution.py:31
  96.7 15.4 %collective-permute-start.5 = (f32[16,8]{0,1:T(8,128)S(1)}, f32[16,8]{0,1:T(8,128)S(1)}, u32[]{:S(2)}, u32[]{:S(2)}) collective-permute-start(f32[16,8]{0,1:T(8,128)S(1)} %add.200), channel_id=1, source_target_pairs={{0,32},{1,33},{2,34},{3,35},{4,36},{5,37},{6,38},{7,39},{8,40},{9,... | collective-permute-start | bytes 1544 | tf_op jit(solution)/shard_map/ppermute | solution.py:31
  117.1 8.0 %collective-permute-start.6 = (f32[16,8]{0,1:T(8,128)S(1)}, f32[16,8]{0,1:T(8,128)S(1)}, u32[]{:S(2)}, u32[]{:S(2)}) collective-permute-start(f32[16,8]{0,1:T(8,128)S(1)} %convolution_bitcast_fusion.3), channel_id=1, source_target_pairs={{0,1},{1,0},{2,3},{3,2},{4,5},{5,4},{6,7},{7,6},{8,9},{9,8},{10,11... | collective-permute-start | bytes 1544 | tf_op jit(solution)/shard_map/ppermute | solution.py:31
  125.1 5.8 %collective-permute-start.7 = (f32[16,8]{0,1:T(8,128)S(1)}, f32[16,8]{0,1:T(8,128)S(1)}, u32[]{:S(2)}, u32[]{:S(2)}) collective-permute-start(f32[16,8]{0,1:T(8,128)S(1)} %add.205), channel_id=1, source_target_pairs={{0,2},{1,3},{2,0},{3,1},{4,6},{5,7},{6,4},{7,5},{8,10},{9,11},{10,... | collective-permute-start | bytes 1544 | tf_op jit(solution)/shard_map/ppermute | solution.py:31
  130.9 4.3 collective-permute-start.8
  135.3 5.2 %collective-permute-start.9 = (f32[16,8]{0,1:T(8,128)S(1)}, f32[16,8]{0,1:T(8,128)S(1)}, u32[]{:S(2)}, u32[]{:S(2)}) collective-permute-start(f32[16,8]{0,1:T(8,128)S(1)} %add.207), channel_id=1, source_target_pairs={{0,8},{1,9},{2,10},{3,11},{4,12},{5,13},{6,14},{7,15},{8,0},{9,1},... | collective-permute-start | bytes 1544 | tf_op jit(solution)/shard_map/ppermute | solution.py:31
  140.5 8.2 %collective-permute-start.10 = (f32[16,8]{0,1:T(8,128)S(1)}, f32[16,8]{0,1:T(8,128)S(1)}, u32[]{:S(2)}, u32[]{:S(2)}) collective-permute-start(f32[16,8]{0,1:T(8,128)S(1)} %add.208), channel_id=1, source_target_pairs={{0,16},{1,17},{2,18},{3,19},{4,20},{5,21},{6,22},{7,23},{8,24},{9,... | collective-permute-start | bytes 1544 | tf_op jit(solution)/shard_map/ppermute | solution.py:31
  148.8 13.1 %collective-permute-start.11 = (f32[16,8]{0,1:T(8,128)S(1)}, f32[16,8]{0,1:T(8,128)S(1)}, u32[]{:S(2)}, u32[]{:S(2)}) collective-permute-start(f32[16,8]{0,1:T(8,128)S(1)} %add.209), channel_id=1, source_target_pairs={{0,32},{1,33},{2,34},{3,35},{4,36},{5,37},{6,38},{7,39},{8,40},{9,... | collective-permute-start | bytes 1544 | tf_op jit(solution)/shard_map/ppermute | solution.py:31
  163.0 34.0 %collective-permute-start.12 = (f32[8,1,128,256]{3,0,2,1:T(8,128)S(1)}, f32[8,1,128,256]{3,0,2,1:T(8,128)S(1)}, u32[]{:S(2)}, u32[]{:S(2)}) collective-permute-start(f32[8,1,128,256]{3,0,2,1:T(8,128)S(1)} %bitcast.55), channel_id=1, source_target_pairs={{1,0},{2,1},{3,2},{4,3},{5,4},{6,5},{7,6},{8,7},{9,8},{10,9},{11,1... | collective-permute-start | bytes 3145736 | tf_op jit(solution)/shard_map/ppermute | solution.py:20
  171.0 26.0 %collective-permute-start.13 = (f32[8,1,128,256]{3,0,2,1:T(8,128)S(1)}, f32[8,1,128,256]{3,0,2,1:T(8,128)S(1)}, u32[]{:S(2)}, u32[]{:S(2)}) collective-permute-start(f32[8,1,128,256]{3,0,2,1:T(8,128)S(1)} %bitcast.56), channel_id=1, source_target_pairs={{0,1},{1,2},{2,3},{3,4},{4,5},{5,6},{6,7},{7,8},{8,9},{9,10},{10,1... | collective-permute-start | bytes 3145736 | tf_op jit(solution)/shard_map/ppermute | solution.py:17
  200.3 3.1 collective-permute-start.14
  203.4 5.8 %collective-permute-start.15 = (f32[16,8]{0,1:T(8,128)S(1)}, f32[16,8]{0,1:T(8,128)S(1)}, u32[]{:S(2)}, u32[]{:S(2)}) collective-permute-start(f32[16,8]{0,1:T(8,128)S(1)} %add.216), channel_id=1, source_target_pairs={{0,2},{1,3},{2,0},{3,1},{4,6},{5,7},{6,4},{7,5},{8,10},{9,11},{10,... | collective-permute-start | bytes 1544 | tf_op jit(solution)/shard_map/ppermute | solution.py:31
  209.2 4.3 collective-permute-start.16
  213.6 5.2 %collective-permute-start.17 = (f32[16,8]{0,1:T(8,128)S(1)}, f32[16,8]{0,1:T(8,128)S(1)}, u32[]{:S(2)}, u32[]{:S(2)}) collective-permute-start(f32[16,8]{0,1:T(8,128)S(1)} %add.218), channel_id=1, source_target_pairs={{0,8},{1,9},{2,10},{3,11},{4,12},{5,13},{6,14},{7,15},{8,0},{9,1},... | collective-permute-start | bytes 1544 | tf_op jit(solution)/shard_map/ppermute | solution.py:31
  218.8 8.2 %collective-permute-start.18 = (f32[16,8]{0,1:T(8,128)S(1)}, f32[16,8]{0,1:T(8,128)S(1)}, u32[]{:S(2)}, u32[]{:S(2)}) collective-permute-start(f32[16,8]{0,1:T(8,128)S(1)} %add.219), channel_id=1, source_target_pairs={{0,16},{1,17},{2,18},{3,19},{4,20},{5,21},{6,22},{7,23},{8,24},{9,... | collective-permute-start | bytes 1544 | tf_op jit(solution)/shard_map/ppermute | solution.py:31
  227.1 13.1 %collective-permute-start.19 = (f32[16,8]{0,1:T(8,128)S(1)}, f32[16,8]{0,1:T(8,128)S(1)}, u32[]{:S(2)}, u32[]{:S(2)}) collective-permute-start(f32[16,8]{0,1:T(8,128)S(1)} %add.220), channel_id=1, source_target_pairs={{0,32},{1,33},{2,34},{3,35},{4,36},{5,37},{6,38},{7,39},{8,40},{9,... | collective-permute-start | bytes 1544 | tf_op jit(solution)/shard_map/ppermute | solution.py:31
  241.4 32.6 %collective-permute-start.20 = (f32[8,1,128,256]{3,0,2,1:T(8,128)S(1)}, f32[8,1,128,256]{3,0,2,1:T(8,128)S(1)}, u32[]{:S(2)}, u32[]{:S(2)}) collective-permute-start(f32[8,1,128,256]{3,0,2,1:T(8,128)S(1)} %bitcast.60), channel_id=1, source_target_pairs={{1,0},{2,1},{3,2},{4,3},{5,4},{6,5},{7,6},{8,7},{9,8},{10,9},{11,1... | collective-permute-start | bytes 3145736 | tf_op jit(solution)/shard_map/ppermute | solution.py:20
  249.2 24.8 %collective-permute-start.21 = (f32[8,1,128,256]{3,0,2,1:T(8,128)S(1)}, f32[8,1,128,256]{3,0,2,1:T(8,128)S(1)}, u32[]{:S(2)}, u32[]{:S(2)}) collective-permute-start(f32[8,1,128,256]{3,0,2,1:T(8,128)S(1)} %bitcast.61), channel_id=1, source_target_pairs={{0,1},{1,2},{2,3},{3,4},{4,5},{5,6},{6,7},{7,8},{8,9},{9,10},{10,1... | collective-permute-start | bytes 3145736 | tf_op jit(solution)/shard_map/ppermute | solution.py:17
  277.3 3.1 collective-permute-start.22
  280.4 5.8 %collective-permute-start.23 = (f32[16,8]{0,1:T(8,128)S(1)}, f32[16,8]{0,1:T(8,128)S(1)}, u32[]{:S(2)}, u32[]{:S(2)}) collective-permute-start(f32[16,8]{0,1:T(8,128)S(1)} %add.228), channel_id=1, source_target_pairs={{0,2},{1,3},{2,0},{3,1},{4,6},{5,7},{6,4},{7,5},{8,10},{9,11},{10,... | collective-permute-start | bytes 1544 | tf_op jit(solution)/shard_map/ppermute | solution.py:31
  286.2 4.3 collective-permute-start.24
  290.6 5.5 %collective-permute-start.25 = (f32[16,8]{0,1:T(8,128)S(1)}, f32[16,8]{0,1:T(8,128)S(1)}, u32[]{:S(2)}, u32[]{:S(2)}) collective-permute-start(f32[16,8]{0,1:T(8,128)S(1)} %add.230), channel_id=1, source_target_pairs={{0,8},{1,9},{2,10},{3,11},{4,12},{5,13},{6,14},{7,15},{8,0},{9,1},... | collective-permute-start | bytes 1544 | tf_op jit(solution)/shard_map/ppermute | solution.py:31
  296.1 8.3 %collective-permute-start.26 = (f32[16,8]{0,1:T(8,128)S(1)}, f32[16,8]{0,1:T(8,128)S(1)}, u32[]{:S(2)}, u32[]{:S(2)}) collective-permute-start(f32[16,8]{0,1:T(8,128)S(1)} %add.231), channel_id=1, source_target_pairs={{0,16},{1,17},{2,18},{3,19},{4,20},{5,21},{6,22},{7,23},{8,24},{9,... | collective-permute-start | bytes 1544 | tf_op jit(solution)/shard_map/ppermute | solution.py:31
  304.4 13.1 %collective-permute-start.27 = (f32[16,8]{0,1:T(8,128)S(1)}, f32[16,8]{0,1:T(8,128)S(1)}, u32[]{:S(2)}, u32[]{:S(2)}) collective-permute-start(f32[16,8]{0,1:T(8,128)S(1)} %add.232), channel_id=1, source_target_pairs={{0,32},{1,33},{2,34},{3,35},{4,36},{5,37},{6,38},{7,39},{8,40},{9,... | collective-permute-start | bytes 1544 | tf_op jit(solution)/shard_map/ppermute | solution.py:31
  318.8 33.5 %collective-permute-start.28 = (f32[8,1,128,256]{3,0,2,1:T(8,128)S(1)}, f32[8,1,128,256]{3,0,2,1:T(8,128)S(1)}, u32[]{:S(2)}, u32[]{:S(2)}) collective-permute-start(f32[8,1,128,256]{3,0,2,1:T(8,128)S(1)} %bitcast.50), channel_id=1, source_target_pairs={{1,0},{2,1},{3,2},{4,3},{5,4},{6,5},{7,6},{8,7},{9,8},{10,9},{11,1... | collective-permute-start | bytes 3145736 | tf_op jit(solution)/shard_map/ppermute | solution.py:20
  326.2 26.0 %collective-permute-start.29 = (f32[8,1,128,256]{3,0,2,1:T(8,128)S(1)}, f32[8,1,128,256]{3,0,2,1:T(8,128)S(1)}, u32[]{:S(2)}, u32[]{:S(2)}) collective-permute-start(f32[8,1,128,256]{3,0,2,1:T(8,128)S(1)} %bitcast.51), channel_id=1, source_target_pairs={{0,1},{1,2},{2,3},{3,4},{4,5},{5,6},{6,7},{7,8},{8,9},{9,10},{10,1... | collective-permute-start | bytes 3145736 | tf_op jit(solution)/shard_map/ppermute | solution.py:17
  352.9 28.8 %copy-start.4 = (s32[2]{0:T(128)S(1)}, s32[2]{0:T(128)}, u32[]{:S(2)}) copy-start(s32[2]{0:T(128)} %param.7) | copy-start | bytes 28
  355.6 3.1 collective-permute-start.30
  358.6 5.8 %collective-permute-start.31 = (f32[16,8]{0,1:T(8,128)S(1)}, f32[16,8]{0,1:T(8,128)S(1)}, u32[]{:S(2)}, u32[]{:S(2)}) collective-permute-start(f32[16,8]{0,1:T(8,128)S(1)} %add.240), channel_id=1, source_target_pairs={{0,2},{1,3},{2,0},{3,1},{4,6},{5,7},{6,4},{7,5},{8,10},{9,11},{10,... | collective-permute-start | bytes 1544 | tf_op jit(solution)/shard_map/ppermute | solution.py:31
  364.5 4.3 collective-permute-start.32
  368.8 5.5 %collective-permute-start.33 = (f32[16,8]{0,1:T(8,128)S(1)}, f32[16,8]{0,1:T(8,128)S(1)}, u32[]{:S(2)}, u32[]{:S(2)}) collective-permute-start(f32[16,8]{0,1:T(8,128)S(1)} %add.242), channel_id=1, source_target_pairs={{0,8},{1,9},{2,10},{3,11},{4,12},{5,13},{6,14},{7,15},{8,0},{9,1},... | collective-permute-start | bytes 1544 | tf_op jit(solution)/shard_map/ppermute | solution.py:31
  374.3 8.3 %collective-permute-start.34 = (f32[16,8]{0,1:T(8,128)S(1)}, f32[16,8]{0,1:T(8,128)S(1)}, u32[]{:S(2)}, u32[]{:S(2)}) collective-permute-start(f32[16,8]{0,1:T(8,128)S(1)} %add.243), channel_id=1, source_target_pairs={{0,16},{1,17},{2,18},{3,19},{4,20},{5,21},{6,22},{7,23},{8,24},{9,... | collective-permute-start | bytes 1544 | tf_op jit(solution)/shard_map/ppermute | solution.py:31
  382.7 13.1 %collective-permute-start.35 = (f32[16,8]{0,1:T(8,128)S(1)}, f32[16,8]{0,1:T(8,128)S(1)}, u32[]{:S(2)}, u32[]{:S(2)}) collective-permute-start(f32[16,8]{0,1:T(8,128)S(1)} %add.244), channel_id=1, source_target_pairs={{0,32},{1,33},{2,34},{3,35},{4,36},{5,37},{6,38},{7,39},{8,40},{9,... | collective-permute-start | bytes 1544 | tf_op jit(solution)/shard_map/ppermute | solution.py:31
  398.0 1.6 copy-start.1
  445.2 4.4 collective-permute-start.36
  449.5 5.8 %collective-permute-start.37 = (f32[4,4]{1,0:T(4,128)S(1)}, f32[4,4]{1,0:T(4,128)S(1)}, u32[]{:S(2)}, u32[]{:S(2)}) collective-permute-start(f32[4,4]{1,0:T(4,128)S(1)} %add.248), channel_id=1, source_target_pairs={{0,128},{64,192},{128,0},{192,64},{256,384},{320,448},{384,256},{4... | collective-permute-start | bytes 200 | tf_op jit(solution)/shard_map/ppermute | solution.py:31
  455.4 4.3 collective-permute-start.38
  459.7 11.8 %collective-permute-start.39 = (f32[4,4]{1,0:T(4,128)S(1)}, f32[4,4]{1,0:T(4,128)S(1)}, u32[]{:S(2)}, u32[]{:S(2)}) collective-permute-start(f32[4,4]{1,0:T(4,128)S(1)} %add.250), channel_id=1, source_target_pairs={{0,1},{1,0},{2,3},{3,2},{4,5},{5,4},{6,7},{7,6},{8,9},{9,8},{10,11... | collective-permute-start | bytes 200 | tf_op jit(solution)/shard_map/ppermute | solution.py:31
  471.5 5.8 %collective-permute-start.40 = (f32[4,4]{1,0:T(4,128)S(1)}, f32[4,4]{1,0:T(4,128)S(1)}, u32[]{:S(2)}, u32[]{:S(2)}) collective-permute-start(f32[4,4]{1,0:T(4,128)S(1)} %add.251), channel_id=1, source_target_pairs={{0,2},{1,3},{2,0},{3,1},{4,6},{5,7},{6,4},{7,5},{8,10},{9,11},{10,... | collective-permute-start | bytes 200 | tf_op jit(solution)/shard_map/ppermute | solution.py:31
  477.4 4.3 collective-permute-start.41
  481.7 5.2 %collective-permute-start.42 = (f32[4,4]{1,0:T(4,128)S(1)}, f32[4,4]{1,0:T(4,128)S(1)}, u32[]{:S(2)}, u32[]{:S(2)}) collective-permute-start(f32[4,4]{1,0:T(4,128)S(1)} %add.253), channel_id=1, source_target_pairs={{0,8},{1,9},{2,10},{3,11},{4,12},{5,13},{6,14},{7,15},{8,0},{9,1},... | collective-permute-start | bytes 200 | tf_op jit(solution)/shard_map/ppermute | solution.py:31
  486.9 8.3 %collective-permute-start.43 = (f32[4,4]{1,0:T(4,128)S(1)}, f32[4,4]{1,0:T(4,128)S(1)}, u32[]{:S(2)}, u32[]{:S(2)}) collective-permute-start(f32[4,4]{1,0:T(4,128)S(1)} %add.254), channel_id=1, source_target_pairs={{0,16},{1,17},{2,18},{3,19},{4,20},{5,21},{6,22},{7,23},{8,24},{9,... | collective-permute-start | bytes 200 | tf_op jit(solution)/shard_map/ppermute | solution.py:31
  495.2 13.4 %collective-permute-start.44 = (f32[4,4]{1,0:T(4,128)S(1)}, f32[4,4]{1,0:T(4,128)S(1)}, u32[]{:S(2)}, u32[]{:S(2)}) collective-permute-start(f32[4,4]{1,0:T(4,128)S(1)} %add.255), channel_id=1, source_target_pairs={{0,32},{1,33},{2,34},{3,35},{4,36},{5,37},{6,38},{7,39},{8,40},{9,... | collective-permute-start | bytes 200 | tf_op jit(solution)/shard_map/ppermute | solution.py:31
Sparse Core Ops, SparseCore 0:
  10.0 48.8 all-gather.2
  401.2 42.7 reduce-scatter.1

commit v2 on v1

v2 whole, which is shorter than its diff:
```python
import math

import jax
import jax.numpy as jnp
from jax import lax
from jax.sharding import PartitionSpec as P

ITERS = 3


def padded_2(block, sides, width):
    for axis, dim in sides:
        count = lax.axis_size(axis)
        forward = [(i, i + 1) for i in range(count - 1)]
        forward.append((count - 1, 0))
        backward = [(target, source) for source, target in forward]
        low = lax.ppermute(
            lax.slice_in_dim(block, block.shape[dim] - width, None, axis=dim), axis, forward
        )
        high = lax.ppermute(lax.slice_in_dim(block, 0, width, axis=dim), axis, backward)
        block = jnp.concatenate([low, block, high], axis=dim)
    return block


def tree_sum(value, axes):
    for axis in axes:
        count = lax.axis_size(axis)
        step = 1
        while step < count:
            pairs = [(i, i ^ step) for i in range(count)]
            value = value + lax.ppermute(value, axis, pairs)
            step *= 2
    return value


def tree_sum_parts(parts, axes):
    flat = jnp.concatenate([part.reshape(-1) for part in parts])
    flat = tree_sum(flat, axes)
    out, start = [], 0
    for part in parts:
        out.append(flat[start : start + part.size].reshape(part.shape))
        start += part.size
    return out


def neighbours_z(field_block):
    z_padded = jnp.pad(field_block, ((0, 0), (0, 0), (0, 0), (1, 1)))
    return z_padded[..., 2:] + z_padded[..., :-2]


def local(orbitals, energies, occupation, potential, trials):
    nb_dev, width_x, width_y, width_z = orbitals.shape
    trial_count = trials.shape[0]
    cell_count = width_x * width_y * width_z
    cell_total = cell_count * lax.axis_size("xy")
    orbital_total = nb_dev * lax.axis_size("band")
    row_count = nb_dev * trial_count
    highest = lax.Precision.HIGHEST

    def dot(a, b):
        return jnp.dot(a, b, precision=highest, preferred_element_type=jnp.float32)

    psi_flat = orbitals.reshape(nb_dev, cell_count)
    trial_flat = trials.reshape(trial_count, cell_count)
    psi_all = lax.all_gather(psi_flat, "band", axis=0, tiled=True)
    weight_rows = occupation.astype(jnp.float32)

    diagonal = 3.0 + potential.reshape(1, cell_count) - energies[:, None]
    diagonal_op = jnp.broadcast_to(
        diagonal[:, None, :], (nb_dev, trial_count, cell_count)
    ).reshape(row_count, cell_count)
    products = (psi_flat[:, None, :] * trial_flat[None, :, :]).reshape(row_count, cell_count)
    products_d = products / diagonal_op

    c0_part = dot(psi_all, products.T)
    cpd_part = dot(psi_all, products_d.T)
    scaled = (psi_all[None, :, :] / diagonal[:, None, :]).reshape(nb_dev * orbital_total, cell_count)
    gram_part = dot(scaled, psi_all.T).reshape(nb_dev, orbital_total, orbital_total)
    c0, cpd, gram = tree_sum_parts((c0_part, cpd_part, gram_part), ("xy",))
    c0 = c0 / cell_total
    cpd = cpd / cell_total
    gram = gram / cell_total

    right_side = dot(c0.T, psi_all) - products
    c0_rows = c0.reshape(orbital_total, nb_dev, trial_count)
    c1 = jnp.einsum("ijl,lik->jik", gram, c0_rows, precision=highest).reshape(
        orbital_total, row_count
    ) - cpd
    update = right_side / diagonal_op - dot(c1.T, psi_all)

    def apply_slab(vectors):
        field_block = vectors.reshape(-1, width_x, width_y, width_z)
        padded = padded_2(field_block, (("xy", 1),), 1)
        beside = padded[:, 2:] + padded[:, :-2]
        beside = beside + jnp.roll(field_block, 1, 2) + jnp.roll(field_block, -1, 2)
        beside = beside + neighbours_z(field_block)
        return diagonal_op * vectors - 0.5 * beside.reshape(vectors.shape)

    for iteration in range(ITERS):
        step = (right_side - apply_slab(update)) / diagonal_op
        if iteration < ITERS - 1:
            (inter,) = tree_sum_parts((dot(psi_all, step.T),), ("xy",))
            update = update + (step - dot((inter / cell_total).T, psi_all))
        else:
            pre = update + step
            pre_rows = pre.reshape(nb_dev, trial_count, cell_count)
            prod_rows = products.reshape(nb_dev, trial_count, cell_count)
            pair_part = jnp.einsum("ikc,ilc->ikl", pre_rows, prod_rows, precision=highest)
            inter, pair = tree_sum_parts((dot(psi_all, step.T), pair_part), ("xy",))
            inter = inter / cell_total
            pair = pair / cell_total
            update = update + (step - dot(inter.T, psi_all))

    inter_rows = inter.reshape(orbital_total, nb_dev, trial_count)
    cross = jnp.einsum("jik,jil->ikl", inter_rows, c0_rows, precision=highest)
    scale = weight_rows / math.sqrt(orbital_total)
    response_part = jnp.einsum("i,ikl->kl", scale, pair - cross, precision=highest)
    (response_matrix,) = tree_sum_parts((response_part,), ("band",))

    weights = weight_rows[:, None, None] * psi_flat[:, None, :]
    summed = jnp.sum(weights * update.reshape(nb_dev, trial_count, cell_count), axis=0)
    partial_grid = (summed / math.sqrt(orbital_total)).reshape(
        trial_count, width_x, width_y, width_z
    )
    density = lax.psum_scatter(partial_grid, "band", scatter_dimension=2, tiled=True)
    return (density, response_matrix)


def solution(mesh):
    in_specs = (
        P("band", "xy", None, None),
        P("band"),
        P("band"),
        P("xy", None, None),
        P(None, "xy", None, None),
    )
    out_specs = (P(None, "xy", "band", None), P())
    return jax.shard_map(local, mesh=mesh, in_specs=in_specs, out_specs=out_specs, check_vma=False)
```

time: 522 us -> 445 us (0.85)
  starting transfers between devices: 247 us -> 178 us
  waiting for transfers between devices: 214 us -> 171 us
  matrix products: 22.8 us -> 42.5 us
  other arithmetic: 4.39 us -> 12.7 us
  local copies, waits for them, and re-layouts: 14 us -> 20.8 us
    ppermute x39 -> x27, starting transfers between devices: 212 us -> 143 us  [tree_sum(): value = value + lax.ppermute(value, axis, pairs)]
    ppermute x39 -> x27, waiting for transfers between devices: 60.2 us -> 36.8 us  [tree_sum(): value = value + lax.ppermute(value, axis, pairs)]
    dot_general x11 -> x15, matrix products: 22.8 us -> 42.5 us  [the longest x11 36 us: dot(): return jnp.dot(a, b, precision=highest, preferred_element_type=jnp.float32)]
    reduce_scatter x1, waiting for transfers between devices: 42 us -> 27.2 us  [local(): lax.psum_scatter(partial_grid, 'band', scatter_dimension=2, tiled=True)]
  transfers between devices with their start and end apart: 47 -> 35, of which waited for: 43 -> 32; matrix products, arithmetic and copies ran while one was open for 2% -> 2% of each run, Pallas kernels for 0% -> 0%
where the time goes in v2:
time: 445 us; the launch traced here: 439 us
  starting transfers between devices  178 us (40%)
  waiting for transfers between devices  171 us (38%)
  matrix products  42.5 us (10%)
  local copies, waits for them, and re-layouts  20.8 us (5%)
  between operations  14.7 us (3%)
  other arithmetic  12.7 us (3%)
    ppermute x27, starting transfers between devices, tree_sum(): value = value + lax.ppermute(value, axis, pairs)  143 us
    ppermute x3, waiting for transfers between devices, padded_2(): lax.ppermute(lax.slice_in_dim(block, 0, width, axis=dim), axis, backward)  62.7 us
    all_gather x1, waiting for transfers between devices, local(): psi_all = lax.all_gather(psi_flat, 'band', axis=0, tiled=True)  44.1 us
    ppermute x27, waiting for transfers between devices, tree_sum(): value = value + lax.ppermute(value, axis, pairs)  36.8 us
    dot_general x11, matrix products, dot(): return jnp.dot(a, b, precision=highest, preferred_element_type=jnp.float32)  36 us
    reduce_scatter x1, waiting for transfers between devices, local(): lax.psum_scatter(partial_grid, 'band', scatter_dimension=2, tiled=True)  27.2 us
    ppermute x3, starting transfers between devices, padded_2(): lax.ppermute(lax.slice_in_dim(block, 0, width, axis=dim), axis, backward)  22.4 us
    ppermute x3, starting transfers between devices, padded_2(): lax.ppermute(lax.slice_in_dim(block, block.shape[dim] - width, None, axis...  12.7 us
  transfers between devices with their start and end apart: 35, of which 32 were waited for; matrix products, arithmetic and copies ran while one was open for 2% of the time, Pallas kernels for 0%

profile of v2, /device:TPU:1, one launch (start us, length us, event | category | flops | bytes accessed | tf_op | source)
XLA Modules:
  0.0 439.5 jit_solution(6503149142192237733)
XLA Ops:
  7.2 1.8 reshape.222
  14.8 44.1 %all-gather.3.cloned.1.call-done = f32[8,2,32768]{2,1,0:T(2,128)} async-done(((f32[1,2,32768]{2,1,0:T(2,128)}), f32[8,2,32768]{2,1,0:T(2,128)}) %all-gather.3.cloned.1.call-update) | async-done | bytes 2097168 | tf_op jit(solution)/shard_map/all_gather | solution.py:65
  58.9 2.7 reshape.223
  61.6 2.3 broadcast_divide_fusion
  63.9 2.5 convolution_bitcast_fusion.4
  66.4 2.6 convolution_bitcast_fusion.3
  69.4 7.1 %fusion.32 = f32[32,16]{1,0:T(8,128)S(1)} fusion(f32[32,32768]{1,0:T(8,128)} %bitcast.73, f32[16,32768]{1,0:T(8,128)S(1)} %reshape.223), kind=kOutput, calls=%fused_computation.75 | convolution fusion | flops 201326592 | bytes 6293504 | tf_op jit(solution)/shard_map/dot_general | solution.py:61
  76.6 7.9 %collective-permute-start = (f32[768]{0:T(1024)S(1)}, f32[768]{0:T(1024)S(1)}, u32[]{:S(2)}, u32[]{:S(2)}) collective-permute-start(f32[768]{0:T(1024)S(1)} %constant_dynamic-update-slice_fusion.4), channel_id=1, source_target_pairs={{0,1},{1,0},{2,3},{3,2},{4,5},{5,4},{6,7},{7,6},{8,9},{9,8},{10,11... | collective-permute-start | bytes 9224 | tf_op jit(solution)/shard_map/ppermute | solution.py:31
  85.3 4.4 collective-permute-start.1
  91.2 3.2 collective-permute-start.2
  95.5 4.2 collective-permute-start.3
  100.7 7.4 %collective-permute-start.4 = (f32[768]{0:T(1024)S(1)}, f32[768]{0:T(1024)S(1)}, u32[]{:S(2)}, u32[]{:S(2)}) collective-permute-start(f32[768]{0:T(1024)S(1)} %add.166), channel_id=1, source_target_pairs={{0,16},{1,17},{2,18},{3,19},{4,20},{5,21},{6,22},{7,23},{8,24},{9,... | collective-permute-start | bytes 9224 | tf_op jit(solution)/shard_map/ppermute | solution.py:31
  109.1 12.6 %collective-permute-start.5 = (f32[768]{0:T(1024)S(1)}, f32[768]{0:T(1024)S(1)}, u32[]{:S(2)}, u32[]{:S(2)}) collective-permute-start(f32[768]{0:T(1024)S(1)} %add.167), channel_id=1, source_target_pairs={{0,32},{1,33},{2,34},{3,35},{4,36},{5,37},{6,38},{7,39},{8,40},{9,... | collective-permute-start | bytes 9224 | tf_op jit(solution)/shard_map/ppermute | solution.py:31
  122.9 3.4 convolution_subtract_fusion.4
  126.6 2.4 convolution_subtract_fusion.3
  129.0 7.7 %collective-permute-start.6 = (f32[8,1,128,256]{3,0,2,1:T(8,128)S(1)}, f32[8,1,128,256]{3,0,2,1:T(8,128)S(1)}, u32[]{:S(2)}, u32[]{:S(2)}) collective-permute-start(f32[8,1,128,256]{3,0,2,1:T(8,128)S(1)} %bitcast.63), channel_id=1, source_target_pairs={{1,0},{2,1},{3,2},{4,3},{5,4},{6,5},{7,6},{8,7},{9,8},{10,9},{11,1... | collective-permute-start | bytes 3145736 | tf_op jit(solution)/shard_map/ppermute | solution.py:20
  136.7 4.2 collective-permute-start.7
  141.1 21.6 %collective-permute-done.6 = f32[8,1,128,256]{3,0,2,1:T(8,128)S(1)} collective-permute-done((f32[8,1,128,256]{3,0,2,1:T(8,128)S(1)}, f32[8,1,128,256]{3,0,2,1:T(8,128)S(1)}, u32[]{:S(2)}, u32[]{:S(2)}) %collective-permute-start.6) | collective-permute-done | bytes 1048608 | tf_op jit(solution)/shard_map/ppermute | solution.py:20
  164.3 2.7 convolution_bitcast_fusion.2
  167.2 1.9 collective-permute-start.8
  170.2 3.7 collective-permute-start.9
  173.9 2.1 collective-permute-done.9
  176.0 3.0 collective-permute-start.10
  180.3 4.0 collective-permute-start.11
  185.5 7.2 %collective-permute-start.12 = (f32[128]{0:T(128)S(1)}, f32[128]{0:T(128)S(1)}, u32[]{:S(2)}, u32[]{:S(2)}) collective-permute-start(f32[128]{0:T(128)S(1)} %add.177), channel_id=1, source_target_pairs={{0,16},{1,17},{2,18},{3,19},{4,20},{5,21},{6,22},{7,23},{8,24},{9,... | collective-permute-start | bytes 1544 | tf_op jit(solution)/shard_map/ppermute | solution.py:31
  193.8 12.4 %collective-permute-start.13 = (f32[128]{0:T(128)S(1)}, f32[128]{0:T(128)S(1)}, u32[]{:S(2)}, u32[]{:S(2)}) collective-permute-start(f32[128]{0:T(128)S(1)} %add.178), channel_id=1, source_target_pairs={{0,32},{1,33},{2,34},{3,35},{4,36},{5,37},{6,38},{7,39},{8,40},{9,... | collective-permute-start | bytes 1544 | tf_op jit(solution)/shard_map/ppermute | solution.py:31
  207.1 3.2 fusion.2
  210.3 7.5 %collective-permute-start.14 = (f32[8,1,128,256]{3,0,2,1:T(8,128)S(1)}, f32[8,1,128,256]{3,0,2,1:T(8,128)S(1)}, u32[]{:S(2)}, u32[]{:S(2)}) collective-permute-start(f32[8,1,128,256]{3,0,2,1:T(8,128)S(1)} %bitcast.68), channel_id=1, source_target_pairs={{1,0},{2,1},{3,2},{4,3},{5,4},{6,5},{7,6},{8,7},{9,8},{10,9},{11,1... | collective-permute-start | bytes 3145736 | tf_op jit(solution)/shard_map/ppermute | solution.py:20
  217.9 4.1 collective-permute-start.15
  222.1 21.6 %collective-permute-done.14 = f32[8,1,128,256]{3,0,2,1:T(8,128)S(1)} collective-permute-done((f32[8,1,128,256]{3,0,2,1:T(8,128)S(1)}, f32[8,1,128,256]{3,0,2,1:T(8,128)S(1)}, u32[]{:S(2)}, u32[]{:S(2)}) %collective-permute-start.14) | collective-permute-done | bytes 1048608 | tf_op jit(solution)/shard_map/ppermute | solution.py:20
  245.4 2.7 convolution_bitcast_fusion.1
  248.2 1.9 collective-permute-start.16
  251.3 3.8 collective-permute-start.17
  255.0 2.0 collective-permute-done.17
  257.1 3.6 collective-permute-start.18
  261.7 4.5 %collective-permute-start.19 = (f32[128]{0:T(128)S(1)}, f32[128]{0:T(128)S(1)}, u32[]{:S(2)}, u32[]{:S(2)}) collective-permute-start(f32[128]{0:T(128)S(1)} %add.188), channel_id=1, source_target_pairs={{0,8},{1,9},{2,10},{3,11},{4,12},{5,13},{6,14},{7,15},{8,0},{9,1},... | collective-permute-start | bytes 1544 | tf_op jit(solution)/shard_map/ppermute | solution.py:31
  267.1 7.4 %collective-permute-start.20 = (f32[128]{0:T(128)S(1)}, f32[128]{0:T(128)S(1)}, u32[]{:S(2)}, u32[]{:S(2)}) collective-permute-start(f32[128]{0:T(128)S(1)} %add.189), channel_id=1, source_target_pairs={{0,16},{1,17},{2,18},{3,19},{4,20},{5,21},{6,22},{7,23},{8,24},{9,... | collective-permute-start | bytes 1544 | tf_op jit(solution)/shard_map/ppermute | solution.py:31
  275.5 10.6 %collective-permute-start.21 = (f32[128]{0:T(128)S(1)}, f32[128]{0:T(128)S(1)}, u32[]{:S(2)}, u32[]{:S(2)}) collective-permute-start(f32[128]{0:T(128)S(1)} %add.190), channel_id=1, source_target_pairs={{0,32},{1,33},{2,34},{3,35},{4,36},{5,37},{6,38},{7,39},{8,40},{9,... | collective-permute-start | bytes 1544 | tf_op jit(solution)/shard_map/ppermute | solution.py:31
  286.1 2.4 collective-permute-done.21
  288.6 3.6 fusion.1
  292.2 7.1 %collective-permute-start.22 = (f32[8,1,128,256]{3,0,2,1:T(8,128)}, f32[8,1,128,256]{3,0,2,1:T(8,128)}, u32[]{:S(2)}, u32[]{:S(2)}) collective-permute-start(f32[8,1,128,256]{3,0,2,1:T(8,128)} %bitcast.11), channel_id=1, source_target_pairs={{1,0},{2,1},{3,2},{4,3},{5,4},{6,5},{7,6},{8,7},{9,8},{10,9},{11,1... | collective-permute-start | bytes 3145736 | tf_op jit(solution)/shard_map/ppermute | solution.py:20
  299.3 4.4 %collective-permute-start.23 = (f32[8,1,128,256]{3,0,2,1:T(8,128)}, f32[8,1,128,256]{3,0,2,1:T(8,128)}, u32[]{:S(2)}, u32[]{:S(2)}) collective-permute-start(f32[8,1,128,256]{3,0,2,1:T(8,128)} %bitcast.11), channel_id=1, source_target_pairs={{0,1},{1,2},{2,3},{3,4},{4,5},{5,6},{6,7},{7,8},{8,9},{9,10},{10,1... | collective-permute-start | bytes 3145736 | tf_op jit(solution)/shard_map/ppermute | solution.py:17
  304.5 1.7 fusion.26
  306.2 19.4 %collective-permute-done.22 = f32[8,1,128,256]{3,0,2,1:T(8,128)} collective-permute-done((f32[8,1,128,256]{3,0,2,1:T(8,128)}, f32[8,1,128,256]{3,0,2,1:T(8,128)}, u32[]{:S(2)}, u32[]{:S(2)}) %collective-permute-start.22) | collective-permute-done | bytes 1048608 | tf_op jit(solution)/shard_map/ppermute | solution.py:20
  325.6 2.9 fusion.11
  328.6 2.8 fusion.25
  331.4 2.6 reshape.216
  334.0 6.0 %fusion.24 = f32[2,4,4]{2,1,0:T(4,128)S(1)} fusion(f32[2,4,32768]{2,1,0:T(4,128)} %reshape.216, f32[4,32768]{1,0:T(4,128)} %bitcast.83, f32[2,32768]{1,0:T(2,128)S(1)} %bitcast.80), kind=kOutput, calls=%fused_computation.67 | convolution fusion | flops 12845056 | bytes 1835136 | tf_op jit(solution)/shard_map/ikc,ilc->ikl/dot_general | solution.py:108
  340.1 2.5 convolution_bitcast_fusion
  342.9 1.9 collective-permute-start.24
  346.0 4.2 collective-permute-start.25
  351.8 3.6 collective-permute-start.26
  356.4 4.5 %collective-permute-start.27 = (f32[160]{0:T(256)S(1)}, f32[160]{0:T(256)S(1)}, u32[]{:S(2)}, u32[]{:S(2)}) collective-permute-start(f32[160]{0:T(256)S(1)} %add.201), channel_id=1, source_target_pairs={{0,8},{1,9},{2,10},{3,11},{4,12},{5,13},{6,14},{7,15},{8,0},{9,1},... | collective-permute-start | bytes 1928 | tf_op jit(solution)/shard_map/ppermute | solution.py:31
  361.9 7.3 %collective-permute-start.28 = (f32[160]{0:T(256)S(1)}, f32[160]{0:T(256)S(1)}, u32[]{:S(2)}, u32[]{:S(2)}) collective-permute-start(f32[160]{0:T(256)S(1)} %add.202), channel_id=1, source_target_pairs={{0,16},{1,17},{2,18},{3,19},{4,20},{5,21},{6,22},{7,23},{8,24},{9,... | collective-permute-start | bytes 1928 | tf_op jit(solution)/shard_map/ppermute | solution.py:31
  370.2 10.6 %collective-permute-start.29 = (f32[160]{0:T(256)S(1)}, f32[160]{0:T(256)S(1)}, u32[]{:S(2)}, u32[]{:S(2)}) collective-permute-start(f32[160]{0:T(256)S(1)} %add.203), channel_id=1, source_target_pairs={{0,32},{1,33},{2,34},{3,35},{4,36},{5,37},{6,38},{7,39},{8,40},{9,... | collective-permute-start | bytes 1928 | tf_op jit(solution)/shard_map/ppermute | solution.py:31
  383.3 3.4 fusion
  386.7 1.6 reshape.218
  390.4 1.9 collective-permute-start.30
  392.3 2.4 collective-permute-done.30
  394.7 3.1 collective-permute-start.31
  397.8 2.7 collective-permute-done.31
  400.5 1.9 collective-permute-start.32
  402.4 2.4 collective-permute-done.32
  405.5 27.2 %reduce-scatter.2.cloned.1.call-done = f32[4,1,16,256]{3,2,1,0:T(8,128)} async-done(((f32[4,1,128,256]{3,2,1,0:T(8,128)}), f32[4,1,16,256]{3,2,1,0:T(8,128)}) %reduce-scatter.2.cloned.1.call-update) | async-done | bytes 65552 | tf_op jit(solution)/shard_map/reduce_scatter | solution.py:125
  (146 shorter events, 38.4 us)
Async XLA Ops:
  7.2 51.8 %all-gather.3.cloned.1.call-start = ((), (), s32[]{:S(2)}) async-start(), calls=%async_computation.2 | async-start | bytes 2359296 | tf_op jit(solution)/shard_map/all_gather | solution.py:65
  9.1 423.6 %reduce-scatter.2.cloned.1.call-start = ((), (), s32[]{:S(2)}) async-start(), calls=%async_computation.1 | async-start | bytes 589824 | tf_op jit(solution)/shard_map/reduce_scatter | solution.py:125
  10.1 1.5 copy-start.13
  11.7 3.1 copy-start.9
  13.2 1.6 copy-start.11
  61.6 2.3 copy-start.5
  76.6 8.7 %collective-permute-start = (f32[768]{0:T(1024)S(1)}, f32[768]{0:T(1024)S(1)}, u32[]{:S(2)}, u32[]{:S(2)}) collective-permute-start(f32[768]{0:T(1024)S(1)} %constant_dynamic-update-slice_fusion.4), channel_id=1, source_target_pairs={{0,1},{1,0},{2,3},{3,2},{4,5},{5,4},{6,7},{7,6},{8,9},{9,8},{10,11... | collective-permute-start | bytes 9224 | tf_op jit(solution)/shard_map/ppermute | solution.py:31
  85.3 5.8 %collective-permute-start.1 = (f32[768]{0:T(1024)S(1)}, f32[768]{0:T(1024)S(1)}, u32[]{:S(2)}, u32[]{:S(2)}) collective-permute-start(f32[768]{0:T(1024)S(1)} %add.163), channel_id=1, source_target_pairs={{0,2},{1,3},{2,0},{3,1},{4,6},{5,7},{6,4},{7,5},{8,10},{9,11},{10,... | collective-permute-start | bytes 9224 | tf_op jit(solution)/shard_map/ppermute | solution.py:31
  91.2 4.3 collective-permute-start.2
  95.5 5.2 %collective-permute-start.3 = (f32[768]{0:T(1024)S(1)}, f32[768]{0:T(1024)S(1)}, u32[]{:S(2)}, u32[]{:S(2)}) collective-permute-start(f32[768]{0:T(1024)S(1)} %add.165), channel_id=1, source_target_pairs={{0,8},{1,9},{2,10},{3,11},{4,12},{5,13},{6,14},{7,15},{8,0},{9,1},... | collective-permute-start | bytes 9224 | tf_op jit(solution)/shard_map/ppermute | solution.py:31
  100.7 8.3 %collective-permute-start.4 = (f32[768]{0:T(1024)S(1)}, f32[768]{0:T(1024)S(1)}, u32[]{:S(2)}, u32[]{:S(2)}) collective-permute-start(f32[768]{0:T(1024)S(1)} %add.166), channel_id=1, source_target_pairs={{0,16},{1,17},{2,18},{3,19},{4,20},{5,21},{6,22},{7,23},{8,24},{9,... | collective-permute-start | bytes 9224 | tf_op jit(solution)/shard_map/ppermute | solution.py:31
  109.1 13.4 %collective-permute-start.5 = (f32[768]{0:T(1024)S(1)}, f32[768]{0:T(1024)S(1)}, u32[]{:S(2)}, u32[]{:S(2)}) collective-permute-start(f32[768]{0:T(1024)S(1)} %add.167), channel_id=1, source_target_pairs={{0,32},{1,33},{2,34},{3,35},{4,36},{5,37},{6,38},{7,39},{8,40},{9,... | collective-permute-start | bytes 9224 | tf_op jit(solution)/shard_map/ppermute | solution.py:31
  129.0 34.4 %copy-start.3 = (f32[8,32768]{1,0:T(8,128)}, f32[8,32768]{1,0:T(8,128)S(1)}, u32[]{:S(2)}) copy-start(f32[8,32768]{1,0:T(8,128)S(1)} %convolution_subtract_fusion.3) | copy-start | bytes 3145732
  129.0 33.7 %collective-permute-start.6 = (f32[8,1,128,256]{3,0,2,1:T(8,128)S(1)}, f32[8,1,128,256]{3,0,2,1:T(8,128)S(1)}, u32[]{:S(2)}, u32[]{:S(2)}) collective-permute-start(f32[8,1,128,256]{3,0,2,1:T(8,128)S(1)} %bitcast.63), channel_id=1, source_target_pairs={{1,0},{2,1},{3,2},{4,3},{5,4},{6,5},{7,6},{8,7},{9,8},{10,9},{11,1... | collective-permute-start | bytes 3145736 | tf_op jit(solution)/shard_map/ppermute | solution.py:20
  136.7 26.0 %collective-permute-start.7 = (f32[8,1,128,256]{3,0,2,1:T(8,128)S(1)}, f32[8,1,128,256]{3,0,2,1:T(8,128)S(1)}, u32[]{:S(2)}, u32[]{:S(2)}) collective-permute-start(f32[8,1,128,256]{3,0,2,1:T(8,128)S(1)} %bitcast.64), channel_id=1, source_target_pairs={{0,1},{1,2},{2,3},{3,4},{4,5},{5,6},{6,7},{7,8},{8,9},{9,10},{10,1... | collective-permute-start | bytes 3145736 | tf_op jit(solution)/shard_map/ppermute | solution.py:17
  162.7 1.6 copy-start
  163.3 1.0 copy-start.7
  167.2 3.1 collective-permute-start.8
  170.2 5.8 %collective-permute-start.9 = (f32[128]{0:T(128)S(1)}, f32[128]{0:T(128)S(1)}, u32[]{:S(2)}, u32[]{:S(2)}) collective-permute-start(f32[128]{0:T(128)S(1)} %add.174), channel_id=1, source_target_pairs={{0,2},{1,3},{2,0},{3,1},{4,6},{5,7},{6,4},{7,5},{8,10},{9,11},{10,... | collective-permute-start | bytes 1544 | tf_op jit(solution)/shard_map/ppermute | solution.py:31
  176.0 4.3 collective-permute-start.10
  180.3 5.2 %collective-permute-start.11 = (f32[128]{0:T(128)S(1)}, f32[128]{0:T(128)S(1)}, u32[]{:S(2)}, u32[]{:S(2)}) collective-permute-start(f32[128]{0:T(128)S(1)} %add.176), channel_id=1, source_target_pairs={{0,8},{1,9},{2,10},{3,11},{4,12},{5,13},{6,14},{7,15},{8,0},{9,1},... | collective-permute-start | bytes 1544 | tf_op jit(solution)/shard_map/ppermute | solution.py:31
  185.5 8.2 %collective-permute-start.12 = (f32[128]{0:T(128)S(1)}, f32[128]{0:T(128)S(1)}, u32[]{:S(2)}, u32[]{:S(2)}) collective-permute-start(f32[128]{0:T(128)S(1)} %add.177), channel_id=1, source_target_pairs={{0,16},{1,17},{2,18},{3,19},{4,20},{5,21},{6,22},{7,23},{8,24},{9,... | collective-permute-start | bytes 1544 | tf_op jit(solution)/shard_map/ppermute | solution.py:31
  193.8 13.3 %collective-permute-start.13 = (f32[128]{0:T(128)S(1)}, f32[128]{0:T(128)S(1)}, u32[]{:S(2)}, u32[]{:S(2)}) collective-permute-start(f32[128]{0:T(128)S(1)} %add.178), channel_id=1, source_target_pairs={{0,32},{1,33},{2,34},{3,35},{4,36},{5,37},{6,38},{7,39},{8,40},{9,... | collective-permute-start | bytes 1544 | tf_op jit(solution)/shard_map/ppermute | solution.py:31
  210.3 34.1 %copy-start.4 = (f32[8,32768]{1,0:T(8,128)}, f32[8,32768]{1,0:T(8,128)S(1)}, u32[]{:S(2)}) copy-start(f32[8,32768]{1,0:T(8,128)S(1)} %fusion.2) | copy-start | bytes 3145732
  210.3 33.4 %collective-permute-start.14 = (f32[8,1,128,256]{3,0,2,1:T(8,128)S(1)}, f32[8,1,128,256]{3,0,2,1:T(8,128)S(1)}, u32[]{:S(2)}, u32[]{:S(2)}) collective-permute-start(f32[8,1,128,256]{3,0,2,1:T(8,128)S(1)} %bitcast.68), channel_id=1, source_target_pairs={{1,0},{2,1},{3,2},{4,3},{5,4},{6,5},{7,6},{8,7},{9,8},{10,9},{11,1... | collective-permute-start | bytes 3145736 | tf_op jit(solution)/shard_map/ppermute | solution.py:20
  217.9 25.9 %collective-permute-start.15 = (f32[8,1,128,256]{3,0,2,1:T(8,128)S(1)}, f32[8,1,128,256]{3,0,2,1:T(8,128)S(1)}, u32[]{:S(2)}, u32[]{:S(2)}) collective-permute-start(f32[8,1,128,256]{3,0,2,1:T(8,128)S(1)} %bitcast.69), channel_id=1, source_target_pairs={{0,1},{1,2},{2,3},{3,4},{4,5},{5,6},{6,7},{7,8},{8,9},{9,10},{10,1... | collective-permute-start | bytes 3145736 | tf_op jit(solution)/shard_map/ppermute | solution.py:17
  243.7 1.6 copy-start.1
  244.4 1.0 copy-start.8
  248.2 3.1 collective-permute-start.16
  251.3 5.8 %collective-permute-start.17 = (f32[128]{0:T(128)S(1)}, f32[128]{0:T(128)S(1)}, u32[]{:S(2)}, u32[]{:S(2)}) collective-permute-start(f32[128]{0:T(128)S(1)} %add.186), channel_id=1, source_target_pairs={{0,2},{1,3},{2,0},{3,1},{4,6},{5,7},{6,4},{7,5},{8,10},{9,11},{10,... | collective-permute-start | bytes 1544 | tf_op jit(solution)/shard_map/ppermute | solution.py:31
  257.1 4.6 %collective-permute-start.18 = (f32[128]{0:T(128)S(1)}, f32[128]{0:T(128)S(1)}, u32[]{:S(2)}, u32[]{:S(2)}) collective-permute-start(f32[128]{0:T(128)S(1)} %add.187), channel_id=1, source_target_pairs={{0,4},{1,5},{2,6},{3,7},{4,0},{5,1},{6,2},{7,3},{8,12},{9,13},{10,... | collective-permute-start | bytes 1544 | tf_op jit(solution)/shard_map/ppermute | solution.py:31
  261.7 5.5 %collective-permute-start.19 = (f32[128]{0:T(128)S(1)}, f32[128]{0:T(128)S(1)}, u32[]{:S(2)}, u32[]{:S(2)}) collective-permute-start(f32[128]{0:T(128)S(1)} %add.188), channel_id=1, source_target_pairs={{0,8},{1,9},{2,10},{3,11},{4,12},{5,13},{6,14},{7,15},{8,0},{9,1},... | collective-permute-start | bytes 1544 | tf_op jit(solution)/shard_map/ppermute | solution.py:31
  267.1 8.3 %collective-permute-start.20 = (f32[128]{0:T(128)S(1)}, f32[128]{0:T(128)S(1)}, u32[]{:S(2)}, u32[]{:S(2)}) collective-permute-start(f32[128]{0:T(128)S(1)} %add.189), channel_id=1, source_target_pairs={{0,16},{1,17},{2,18},{3,19},{4,20},{5,21},{6,22},{7,23},{8,24},{9,... | collective-permute-start | bytes 1544 | tf_op jit(solution)/shard_map/ppermute | solution.py:31
  275.5 13.0 %collective-permute-start.21 = (f32[128]{0:T(128)S(1)}, f32[128]{0:T(128)S(1)}, u32[]{:S(2)}, u32[]{:S(2)}) collective-permute-start(f32[128]{0:T(128)S(1)} %add.190), channel_id=1, source_target_pairs={{0,32},{1,33},{2,34},{3,35},{4,36},{5,37},{6,38},{7,39},{8,40},{9,... | collective-permute-start | bytes 1544 | tf_op jit(solution)/shard_map/ppermute | solution.py:31
  292.2 33.5 %collective-permute-start.22 = (f32[8,1,128,256]{3,0,2,1:T(8,128)}, f32[8,1,128,256]{3,0,2,1:T(8,128)}, u32[]{:S(2)}, u32[]{:S(2)}) collective-permute-start(f32[8,1,128,256]{3,0,2,1:T(8,128)} %bitcast.11), channel_id=1, source_target_pairs={{1,0},{2,1},{3,2},{4,3},{5,4},{6,5},{7,6},{8,7},{9,8},{10,9},{11,1... | collective-permute-start | bytes 3145736 | tf_op jit(solution)/shard_map/ppermute | solution.py:20
  299.3 26.3 %collective-permute-start.23 = (f32[8,1,128,256]{3,0,2,1:T(8,128)}, f32[8,1,128,256]{3,0,2,1:T(8,128)}, u32[]{:S(2)}, u32[]{:S(2)}) collective-permute-start(f32[8,1,128,256]{3,0,2,1:T(8,128)} %bitcast.11), channel_id=1, source_target_pairs={{0,1},{1,2},{2,3},{3,4},{4,5},{5,6},{6,7},{7,8},{8,9},{9,10},{10,1... | collective-permute-start | bytes 3145736 | tf_op jit(solution)/shard_map/ppermute | solution.py:17
  325.6 3.0 copy-start.2
  331.4 2.6 copy-start.10
  331.4 8.8 %copy-start.6 = (f32[8,32768]{1,0:T(8,128)S(1)}, f32[8,32768]{1,0:T(8,128)}, u32[]{:S(2)}) copy-start(f32[8,32768]{1,0:T(8,128)} %get-tuple-element.3) | copy-start | bytes 3145732
  334.0 35.2 %copy-start.14 = (s32[2]{0:T(128)S(1)}, s32[2]{0:T(128)}, u32[]{:S(2)}) copy-start(s32[2]{0:T(128)} %param.7) | copy-start | bytes 28
  342.9 3.0 collective-permute-start.24
  346.0 5.8 %collective-permute-start.25 = (f32[160]{0:T(256)S(1)}, f32[160]{0:T(256)S(1)}, u32[]{:S(2)}, u32[]{:S(2)}) collective-permute-start(f32[160]{0:T(256)S(1)} %add.199), channel_id=1, source_target_pairs={{0,2},{1,3},{2,0},{3,1},{4,6},{5,7},{6,4},{7,5},{8,10},{9,11},{10,... | collective-permute-start | bytes 1928 | tf_op jit(solution)/shard_map/ppermute | solution.py:31
  351.8 4.6 %collective-permute-start.26 = (f32[160]{0:T(256)S(1)}, f32[160]{0:T(256)S(1)}, u32[]{:S(2)}, u32[]{:S(2)}) collective-permute-start(f32[160]{0:T(256)S(1)} %add.200), channel_id=1, source_target_pairs={{0,4},{1,5},{2,6},{3,7},{4,0},{5,1},{6,2},{7,3},{8,12},{9,13},{10,... | collective-permute-start | bytes 1928 | tf_op jit(solution)/shard_map/ppermute | solution.py:31
  356.4 5.5 %collective-permute-start.27 = (f32[160]{0:T(256)S(1)}, f32[160]{0:T(256)S(1)}, u32[]{:S(2)}, u32[]{:S(2)}) collective-permute-start(f32[160]{0:T(256)S(1)} %add.201), channel_id=1, source_target_pairs={{0,8},{1,9},{2,10},{3,11},{4,12},{5,13},{6,14},{7,15},{8,0},{9,1},... | collective-permute-start | bytes 1928 | tf_op jit(solution)/shard_map/ppermute | solution.py:31
  361.9 8.3 %collective-permute-start.28 = (f32[160]{0:T(256)S(1)}, f32[160]{0:T(256)S(1)}, u32[]{:S(2)}, u32[]{:S(2)}) collective-permute-start(f32[160]{0:T(256)S(1)} %add.202), channel_id=1, source_target_pairs={{0,16},{1,17},{2,18},{3,19},{4,20},{5,21},{6,22},{7,23},{8,24},{9,... | collective-permute-start | bytes 1928 | tf_op jit(solution)/shard_map/ppermute | solution.py:31
  370.2 13.0 %collective-permute-start.29 = (f32[160]{0:T(256)S(1)}, f32[160]{0:T(256)S(1)}, u32[]{:S(2)}, u32[]{:S(2)}) collective-permute-start(f32[160]{0:T(256)S(1)} %add.203), channel_id=1, source_target_pairs={{0,32},{1,33},{2,34},{3,35},{4,36},{5,37},{6,38},{7,39},{8,40},{9,... | collective-permute-start | bytes 1928 | tf_op jit(solution)/shard_map/ppermute | solution.py:31
  386.7 1.6 copy-start.12
  390.4 4.3 collective-permute-start.30
  394.7 5.8 %collective-permute-start.31 = (f32[16]{0:T(128)S(1)}, f32[16]{0:T(128)S(1)}, u32[]{:S(2)}, u32[]{:S(2)}) collective-permute-start(f32[16]{0:T(128)S(1)} %add.206), channel_id=1, source_target_pairs={{0,128},{64,192},{128,0},{192,64},{256,384},{320,448},{384,256},{4... | collective-permute-start | bytes 200 | tf_op jit(solution)/shard_map/ppermute | solution.py:31
  400.5 4.3 collective-permute-start.32
Sparse Core Ops, SparseCore 0:
  10.0 48.8 all-gather.2
  389.8 42.7 reduce-scatter.1
